TPU v7x, 512 devices: a whole 4x4x16 slice. The times are simulated.
512 devices in a mesh: row: 32 (over z, core), col: 16 (over y, x).
Axes of the slice: x: 4, y: 4, z: 16, core: 2. Of those that a mesh axis runs over, the one named last changes fastest.
Arguments:
- tokens: bfloat16 [512, 8192], P('row', 'col'), may hold values from -6 to 6
- out_grad: bfloat16 [512, 8192], P('row', 'col'), may hold values from -1.5 to 1.5
- gate_weight: bfloat16 [8192, 16384], P('col', 'row'), may hold values from -0.0625 to 0.0625
- up_weight: bfloat16 [8192, 16384], P('col', 'row'), may hold values from -0.0625 to 0.0625
- down_weight: bfloat16 [16384, 8192], P('row', 'col'), may hold values from -0.046875 to 0.046875
Outputs:
- input_grad: bfloat16 [512, 8192], P('row', 'col')
- gate_weight_grad: bfloat16 [8192, 16384], P('col', 'row')
- up_weight_grad: bfloat16 [8192, 16384], P('col', 'row')
- down_weight_grad: bfloat16 [16384, 8192], P('row', 'col')
All inputs are finite; a program needn't handle non-finite values.
Results may differ from a plain program's by a relative error of at most 0.005.
Values may be sent and summed in bfloat16 or wider, within the bound.
No kernel may reach another device: no remote copies, remote signals or barrier semaphores. Data moves between devices by JAX's collectives and lax.ppermute only.
A program may use at most 64 MiB of HBM per device.

v0:
```python
import jax
import jax.numpy as jnp
from jax import lax
from jax.sharding import PartitionSpec as P


def pointwise(gate, up, hidden_grad):
    sig = jax.nn.sigmoid(gate)
    act = gate * sig
    hidden = (act * up).astype(jnp.bfloat16)
    gate_grad = (hidden_grad * up * sig * (1.0 + gate * (1.0 - sig))).astype(jnp.bfloat16)
    up_grad = (hidden_grad * act).astype(jnp.bfloat16)
    return (hidden, gate_grad, up_grad)


def body(tokens, out_grad, gate_weight, up_weight, down_weight):
    rows_all, grads_all = (
        lax.all_gather(tokens, "row", axis=0, tiled=True),
        lax.all_gather(out_grad, "row", axis=0, tiled=True),
    )
    contract_cols = (((1,), (1,)), ((), ()))
    contract_rows = (((0,), (0,)), ((), ()))
    gate_part = jnp.dot(rows_all, gate_weight, preferred_element_type=jnp.float32)
    up_part = jnp.dot(rows_all, up_weight, preferred_element_type=jnp.float32)
    grad_part = lax.dot_general(
        grads_all, down_weight, contract_cols, preferred_element_type=jnp.float32
    )
    gate, up, hidden_grad = lax.psum((gate_part, up_part, grad_part), "col")
    hidden, gate_grad, up_grad = pointwise(gate, up, hidden_grad)
    gate_weight_grad = lax.dot_general(
        rows_all, gate_grad, contract_rows, preferred_element_type=jnp.float32
    ).astype(jnp.bfloat16)
    up_weight_grad = lax.dot_general(
        rows_all, up_grad, contract_rows, preferred_element_type=jnp.float32
    ).astype(jnp.bfloat16)
    down_weight_grad = lax.dot_general(
        hidden, grads_all, contract_rows, preferred_element_type=jnp.float32
    ).astype(jnp.bfloat16)
    total = lax.dot_general(
        gate_grad, gate_weight, contract_cols, preferred_element_type=jnp.float32
    )
    input_grad = lax.psum_scatter(
        total
        + lax.dot_general(up_grad, up_weight, contract_cols, preferred_element_type=jnp.float32),
        "row",
        scatter_dimension=0,
        tiled=True,
    )
    return (input_grad.astype(jnp.bfloat16), gate_weight_grad, up_weight_grad, down_weight_grad)


def solution(mesh):
    return jax.shard_map(
        body,
        mesh=mesh,
        in_specs=(
            P("row", "col"),
            P("row", "col"),
            P("col", "row"),
            P("col", "row"),
            P("row", "col"),
        ),
        out_specs=(P("row", "col"), P("col", "row"), P("col", "row"), P("row", "col")),
        check_vma=False,
    )
```

profile of v0, /device:TPU:2, one launch (start us, length us, event | category | flops | bytes accessed | tf_op | source)
XLA Modules:
  0.0 323.2 jit_solution(6330237184376752438)
XLA Ops:
  7.2 0.0 copy-start
  7.2 0.0 copy-start.4
  7.2 0.0 all-reduce.3.cloned.1.call-start
  7.2 38.0 %all_gather.7 = bf16[512,512]{1,0:T(8,128)(2,1)S(1)} all-gather(bf16[16,512]{1,0:T(8,128)(2,1)} %param.5), channel_id=1, replica_groups=mesh['row'=32,'col'=16] {'row'}, dimensions={0}, use_global_device_ids=true | all-gather | bytes 540672 | tf_op jit(solution)/shard_map/all_gather | solution.py:18
  45.3 0.0 copy-done.4
  45.3 28.5 %all_gather.6 = bf16[512,512]{1,0:T(8,128)(2,1)S(1)} all-gather(bf16[16,512]{1,0:T(8,128)(2,1)S(1)} %copy-done.4), channel_id=1, replica_groups=mesh['row'=32,'col'=16] {'row'}, dimensions={0}, use_global_device_ids=true | all-gather | bytes 540672 | tf_op jit(solution)/shard_map/all_gather | solution.py:19
  73.8 0.0 copy-done
  73.8 0.0 copy-start.1
  73.8 1.4 fusion.7
  75.2 0.0 copy-done.1
  75.2 0.0 copy-start.3
  75.2 1.4 fusion.6
  76.7 0.0 copy-done.3
  76.7 1.4 fusion.5
  78.1 0.0 all-reduce.3.cloned.1.call-update
  78.1 0.0 reduce-scatter.2.cloned.1.call-start
  78.2 122.5 %all-reduce.3.cloned.1.call-done = (f32[512,512]{1,0:T(8,128)}, f32[512,512]{1,0:T(8,128)}, f32[512,512]{1,0:T(8,128)}) async-done(((f32[512,512]{1,0:T(8,128)}, f32[512,512]{1,0:T(8,128)}, f32[512,512]{1,0:T(8,128)}), (f32[512,512]{1,0:T(8,128)}, f32[512,512]{1,0:T(8,128)}, f32[512,512]{1,0:T(8,128)})) %all-reduce.3.cloned.1.call-update) | async-done | bytes 3145744 | tf_op jit(solution)/shard_map/psum | solution.py:28
  200.7 2.5 multiply_convert_fusion.1
  203.1 0.5 fusion.8
  203.6 1.5 convolution_add_fusion
  205.1 0.0 reduce-scatter.2.cloned.1.call-update
  205.1 0.5 fusion
  205.5 1.0 copy.9
  206.6 0.5 fusion.1
  207.0 0.0 copy-start.2
  207.0 1.0 copy.10
  208.0 0.4 copy-done.2
  208.4 2.5 convolution_convert_fusion
  211.0 104.1 %reduce-scatter.2.cloned.1.call-done = f32[16,512]{1,0:T(8,128)} async-done(((f32[512,512]{1,0:T(8,128)}), f32[16,512]{1,0:T(8,128)}) %reduce-scatter.2.cloned.1.call-update) | async-done | bytes 32784 | tf_op jit(solution)/shard_map/reduce_scatter | solution.py:42
  315.0 1.4 convert_element_type.29
Async XLA Ops:
  7.2 66.6 %copy-start = (bf16[512,512]{1,0:T(8,128)(2,1)S(1)}, bf16[512,512]{1,0:T(8,128)(2,1)}, u32[]{:S(2)}) copy-start(bf16[512,512]{1,0:T(8,128)(2,1)} %param.7) | copy-start | bytes 1572868
  7.2 38.1 %copy-start.4 = (bf16[16,512]{1,0:T(8,128)(2,1)S(1)}, bf16[16,512]{1,0:T(8,128)(2,1)}, u32[]{:S(2)}) copy-start(bf16[16,512]{1,0:T(8,128)(2,1)} %param.6) | copy-start | bytes 49156
  7.2 193.5 %all-reduce.3.cloned.1.call-start = ((), (), s32[]{:S(2)}) async-start(), calls=%async_computation.2 | async-start | bytes 6291456 | tf_op jit(solution)/shard_map/psum | solution.py:28
  73.8 1.4 copy-start.1
  75.2 1.5 copy-start.3
  78.1 236.9 %reduce-scatter.2.cloned.1.call-start = ((), (), s32[]{:S(2)}) async-start(), calls=%async_computation.1 | async-start | bytes 1081344 | tf_op jit(solution)/shard_map/reduce_scatter | solution.py:42
  207.0 1.4 copy-start.2
Sparse Core Ops, SparseCore 0:
  78.2 122.3 all-reduce.2
  205.2 109.7 reduce-scatter.1
where the time goes:
time: 324 us; the launch traced here: 323 us
  waiting for transfers between devices  227 us (70%)
  blocking collectives  66.5 us (21%)
  between operations  14.1 us (4%)
  matrix products  9.67 us (3%)
  other arithmetic  3.82 us (1%)
    psum x1, waiting for transfers between devices, body(): gate, up, hidden_grad = lax.psum((gate_part, up_part, grad_part), 'col')  122 us
    reduce_scatter x1, waiting for transfers between devices, body(): lax.psum_scatter(total + lax.dot_general(up_grad, up_weight, contract_col...  104 us
    all_gather x1, blocking collectives, body(): lax.all_gather(tokens, 'row', axis=0, tiled=True)  38 us
    all_gather x1, blocking collectives, body(): lax.all_gather(out_grad, 'row', axis=0, tiled=True)  28.5 us
  transfers between devices with their start and end apart: 2, of which 2 were waited for; matrix products, arithmetic and copies ran while one was open for 2% of the time, Pallas kernels for 0%

commit v1 on v0

--- a/solution.py
+++ b/solution.py
@@ -14,10 +14,11 @@
 
 
 def body(tokens, out_grad, gate_weight, up_weight, down_weight):
-    rows_all, grads_all = (
-        lax.all_gather(tokens, "row", axis=0, tiled=True),
-        lax.all_gather(out_grad, "row", axis=0, tiled=True),
-    )
+    n_col = lax.psum(1, "col")
+    n_row = lax.psum(1, "row")
+    rows_all = lax.all_gather(tokens, "row", axis=0, tiled=True)
+    grads_all = lax.all_gather(out_grad, "row", axis=0, tiled=True)
+    n_tok, width = rows_all.shape
     contract_cols = (((1,), (1,)), ((), ()))
     contract_rows = (((0,), (0,)), ((), ()))
     gate_part = jnp.dot(rows_all, gate_weight, preferred_element_type=jnp.float32)
@@ -25,8 +26,16 @@
     grad_part = lax.dot_general(
         grads_all, down_weight, contract_cols, preferred_element_type=jnp.float32
     )
-    gate, up, hidden_grad = lax.psum((gate_part, up_part, grad_part), "col")
-    hidden, gate_grad, up_grad = pointwise(gate, up, hidden_grad)
+    hid = gate_part.shape[1]
+    chunk = n_tok // n_col
+    parts = jnp.stack([gate_part, up_part, grad_part]).reshape(3, n_col, chunk, hid)
+    parts = lax.all_to_all(parts, "col", 1, 1, tiled=True)
+    gate, up, hidden_grad = parts.sum(axis=1)
+    small = jnp.stack(pointwise(gate, up, hidden_grad))
+    spread = jnp.broadcast_to(small[None], (n_col,) + small.shape)
+    spread = lax.all_to_all(spread, "col", 0, 0, tiled=True)
+    spread = spread.transpose(1, 0, 2, 3).reshape(3, n_tok, hid)
+    hidden, gate_grad, up_grad = spread[0], spread[1], spread[2]
     gate_weight_grad = lax.dot_general(
         rows_all, gate_grad, contract_rows, preferred_element_type=jnp.float32
     ).astype(jnp.bfloat16)
@@ -38,14 +47,9 @@
     ).astype(jnp.bfloat16)
     total = lax.dot_general(
         gate_grad, gate_weight, contract_cols, preferred_element_type=jnp.float32
-    )
-    input_grad = lax.psum_scatter(
-        total
-        + lax.dot_general(up_grad, up_weight, contract_cols, preferred_element_type=jnp.float32),
-        "row",
-        scatter_dimension=0,
-        tiled=True,
-    )
+    ) + lax.dot_general(up_grad, up_weight, contract_cols, preferred_element_type=jnp.float32)
+    total = total.reshape(n_row, n_tok // n_row, width)
+    input_grad = lax.all_to_all(total, "row", 0, 0, tiled=True).sum(axis=0)
     return (input_grad.astype(jnp.bfloat16), gate_weight_grad, up_weight_grad, down_weight_grad)
 
 

time: 324 us -> 214 us (0.66)
  the two profiles are of different devices: /device:TPU:2 before, /device:TPU:1 now
where the time goes in v1:
time: 214 us; the launch traced here: 213 us
  blocking collectives  138 us (64%)
  waiting for transfers between devices  45.8 us (21%)
  matrix products  10.1 us (5%)
  starting transfers between devices  9.62 us (4%)
  local copies, waits for them, and re-layouts  5.2 us (2%)
  other arithmetic  3.47 us (2%)
    all_to_all x1, waiting for transfers between devices, body(): input_grad = lax.all_to_all(total, 'row', 0, 0, tiled=True).sum(axis=0)  45.8 us
    all_to_all x1, blocking collectives, body(): parts = lax.all_to_all(parts, 'col', 1, 1, tiled=True)  45.6 us
    all_gather x1, blocking collectives, body(): rows_all = lax.all_gather(tokens, 'row', axis=0, tiled=True)  39.4 us
    all_gather x1, blocking collectives, body(): grads_all = lax.all_gather(out_grad, 'row', axis=0, tiled=True)  28.7 us
    all_to_all x1, blocking collectives, body(): spread = lax.all_to_all(spread, 'col', 0, 0, tiled=True)  24.6 us
    all_to_all x1, starting transfers between devices, body(): input_grad = lax.all_to_all(total, 'row', 0, 0, tiled=True).sum(axis=0)  9.62 us
  transfers between devices with their start and end apart: 1, of which 1 were waited for; matrix products, arithmetic and copies ran while one was open for 5% of the time, Pallas kernels for 0%

profile of v1, /device:TPU:1, one launch (start us, length us, event | category | flops | bytes accessed | tf_op | source)
XLA Modules:
  0.0 213.3 jit_solution(18360959105764189668)
XLA Ops:
  0.6 0.0 copy-start
  0.6 0.0 copy-start.3
  0.7 39.4 %all_gather.6 = bf16[512,512]{1,0:T(8,128)(2,1)S(1)} all-gather(bf16[16,512]{1,0:T(8,128)(2,1)} %param.5), channel_id=1, replica_groups=mesh['row'=32,'col'=16] {'row'}, dimensions={0}, use_global_device_ids=true | all-gather | bytes 540672 | tf_op jit(solution)/shard_map/all_gather | solution.py:19
  40.0 28.7 %all_gather.7 = bf16[512,512]{1,0:T(8,128)(2,1)S(1)} all-gather(bf16[16,512]{1,0:T(8,128)(2,1)} %param.6), channel_id=1, replica_groups=mesh['row'=32,'col'=16] {'row'}, dimensions={0}, use_global_device_ids=true | all-gather | bytes 540672 | tf_op jit(solution)/shard_map/all_gather | solution.py:20
  68.8 1.5 fusion.5
  70.3 0.0 copy-done
  70.3 0.4 fusion.4
  70.7 0.0 copy-done.3
  70.7 0.5 fusion.6
  71.2 0.5 pad_maximum_fusion
  71.7 45.6 %all_to_all.15 = f32[3,16,32,512]{3,2,0,1:T(8,128)} all-to-all(f32[3,16,32,512]{3,2,0,1:T(8,128)S(1)} %pad_maximum_fusion), channel_id=1, replica_groups=mesh['row'=32,'col'=16] {'col'}, dimensions={1} | all-to-all | bytes 6291456 | tf_op jit(solution)/shard_map/all_to_all | solution.py:32
  117.4 2.2 %reduce_sum.18 = f32[3,32,512]{2,1,0:T(8,128)S(1)} reduce(f32[3,16,32,512]{3,2,0,1:T(8,128)} %all_to_all.15, f32[]{:T(128)} %constant.0.clone.1), dimensions={1}, to_apply=%region_0.0 | reduce | flops 737280 | bytes 3342340 | tf_op jit(solution)/shard_map/reduce_sum | solution.py:33
  119.6 0.2 broadcast_in_dim.2
  119.8 24.6 %all_to_all.16 = bf16[16,3,32,512]{3,2,1,0:T(8,128)(2,1)S(1)} all-to-all(bf16[16,3,32,512]{3,2,1,0:T(8,128)(2,1)S(1)} %broadcast_in_dim.2), channel_id=1, replica_groups=mesh['row'=32,'col'=16] {'col'}, dimensions={0} | all-to-all | bytes 3145728 | tf_op jit(solution)/shard_map/all_to_all | solution.py:36
  144.4 0.0 copy-start.1
  144.4 0.9 fusion.3
  145.3 0.0 copy-start.2
  145.3 0.5 fusion.7
  145.8 0.0 copy-done.1
  145.8 1.4 convolution_add_fusion
  147.3 0.0 copy-done.2
  147.3 9.6 %all-to-all-start.2 = ((f32[32,16,512]{2,1,0:T(8,128)}), f32[32,16,512]{2,1,0:T(8,128)S(1)}, u32[]{:S(2)}, u32[]{:S(2)}) async-start(f32[32,16,512]{2,1,0:T(8,128)} %bitcast.9), calls=%async_computation.2 | async-start | bytes 2097152 | tf_op jit(solution)/shard_map/all_to_all | solution.py:52
  156.9 2.3 %fusion = bf16[512,512]{0,1:T(8,128)(2,1)} fusion(bf16[512,512]{1,0:T(8,128)(2,1)} %bitcast.41, bf16[512,512]{1,0:T(8,128)(2,1)S(1)} %all_gather.6), kind=kOutput, calls=%fused_computation.5 | convolution fusion | flops 268697600 | bytes 1572864 | tf_op jit(solution)/shard_map/dot_general | solution.py:39
  159.2 2.0 copy.14
  161.2 1.3 fusion.1
  162.5 2.0 copy.15
  164.5 2.3 %convolution_convert_fusion = bf16[512,512]{1,0:T(8,128)(2,1)} fusion(bf16[512,512]{1,0:T(8,128)(2,1)} %bitcast.42, bf16[512,512]{1,0:T(8,128)(2,1)S(1)} %all_gather.7), kind=kOutput, calls=%fused_computation.2 | convolution fusion | flops 268697600 | bytes 1572864 | tf_op jit(solution)/shard_map/dot_general | solution.py:45
  166.8 45.8 %all-to-all-done.2 = f32[32,16,512]{2,1,0:T(8,128)S(1)} async-done(((f32[32,16,512]{2,1,0:T(8,128)}), f32[32,16,512]{2,1,0:T(8,128)S(1)}, u32[]{:S(2)}, u32[]{:S(2)}) %all-to-all-start.2) | async-done | bytes 1048608 | tf_op jit(solution)/shard_map/all_to_all | solution.py:52
  212.6 0.7 reduce_sum.19
  (2 shorter events, 0.1 us)
Async XLA Ops:
  0.6 69.6 %copy-start = (bf16[512,512]{1,0:T(8,128)(2,1)S(1)}, bf16[512,512]{1,0:T(8,128)(2,1)}, u32[]{:S(2)}) copy-start(bf16[512,512]{1,0:T(8,128)(2,1)} %param.7) | copy-start | bytes 1572868
  0.6 70.1 %copy-start.3 = (bf16[512,512]{1,0:T(8,128)(2,1)S(1)}, bf16[512,512]{1,0:T(8,128)(2,1)}, u32[]{:S(2)}) copy-start(bf16[512,512]{1,0:T(8,128)(2,1)} %param.9) | copy-start | bytes 1572868
  144.4 1.4 copy-start.1
  145.3 1.9 copy-start.2
  147.3 65.3 %all-to-all-start.2 = ((f32[32,16,512]{2,1,0:T(8,128)}), f32[32,16,512]{2,1,0:T(8,128)S(1)}, u32[]{:S(2)}, u32[]{:S(2)}) async-start(f32[32,16,512]{2,1,0:T(8,128)} %bitcast.9), calls=%async_computation.2 | async-start | bytes 2097152 | tf_op jit(solution)/shard_map/all_to_all | solution.py:52

commit v2 on v1

--- a/solution.py
+++ b/solution.py
@@ -1,7 +1,9 @@
 import jax
 import jax.numpy as jnp
 from jax import lax
-from jax.sharding import PartitionSpec as P
+from jax.sharding import Mesh, PartitionSpec as P
+
+ROW = ("z", "core")
 
 
 def pointwise(gate, up, hidden_grad):
@@ -15,9 +17,10 @@
 
 def body(tokens, out_grad, gate_weight, up_weight, down_weight):
     n_col = lax.psum(1, "col")
-    n_row = lax.psum(1, "row")
-    rows_all = lax.all_gather(tokens, "row", axis=0, tiled=True)
-    grads_all = lax.all_gather(out_grad, "row", axis=0, tiled=True)
+    n_z = lax.psum(1, "z")
+    n_core = lax.psum(1, "core")
+    rows_all = lax.all_gather(tokens, ROW, axis=0, tiled=True)
+    grads_all = lax.all_gather(out_grad, ROW, axis=0, tiled=True)
     n_tok, width = rows_all.shape
     contract_cols = (((1,), (1,)), ((), ()))
     contract_rows = (((0,), (0,)), ((), ()))
@@ -48,22 +51,26 @@
     total = lax.dot_general(
         gate_grad, gate_weight, contract_cols, preferred_element_type=jnp.float32
     ) + lax.dot_general(up_grad, up_weight, contract_cols, preferred_element_type=jnp.float32)
-    total = total.reshape(n_row, n_tok // n_row, width)
-    input_grad = lax.all_to_all(total, "row", 0, 0, tiled=True).sum(axis=0)
+    block = n_tok // (n_z * n_core)
+    total = total.reshape(n_z, n_core, block, width).transpose(1, 0, 2, 3)
+    total = lax.all_to_all(total, "core", 0, 0, tiled=True).sum(axis=0)
+    input_grad = lax.all_to_all(total, "z", 0, 0, tiled=True).sum(axis=0)
     return (input_grad.astype(jnp.bfloat16), gate_weight_grad, up_weight_grad, down_weight_grad)
 
 
 def solution(mesh):
+    n_row, n_col = mesh.shape["row"], mesh.shape["col"]
+    split = Mesh(mesh.devices.reshape(n_row // 2, 2, n_col), ("z", "core", "col"))
     return jax.shard_map(
         body,
-        mesh=mesh,
+        mesh=split,
         in_specs=(
-            P("row", "col"),
-            P("row", "col"),
-            P("col", "row"),
-            P("col", "row"),
-            P("row", "col"),
+            P(ROW, "col"),
+            P(ROW, "col"),
+            P("col", ROW),
+            P("col", ROW),
+            P(ROW, "col"),
         ),
-        out_specs=(P("row", "col"), P("col", "row"), P("col", "row"), P("row", "col")),
+        out_specs=(P(ROW, "col"), P("col", ROW), P("col", ROW), P(ROW, "col")),
         check_vma=False,
     )

time: 214 us -> 191 us (0.89)
  the two profiles are of different devices: /device:TPU:1 before, /device:TPU:32 now
where the time goes in v2:
time: 191 us; the launch traced here: 190 us
  blocking collectives  143 us (75%)
  waiting for transfers between devices  23.1 us (12%)
  starting transfers between devices  7.64 us (4%)
  matrix products  7.57 us (4%)
  other arithmetic  4.35 us (2%)
  local copies, waits for them, and re-layouts  3.21 us (2%)
    all_to_all x1, blocking collectives, body(): parts = lax.all_to_all(parts, 'col', 1, 1, tiled=True)  47.1 us
    all_gather x1, blocking collectives, body(): rows_all = lax.all_gather(tokens, ROW, axis=0, tiled=True)  35.9 us
    all_gather x1, blocking collectives, body(): grads_all = lax.all_gather(out_grad, ROW, axis=0, tiled=True)  30.6 us
    all_to_all x1, blocking collectives, body(): spread = lax.all_to_all(spread, 'col', 0, 0, tiled=True)  25.2 us
    all_to_all x1, waiting for transfers between devices, body(): input_grad = lax.all_to_all(total, 'z', 0, 0, tiled=True).sum(axis=0)  23.1 us
    all_to_all x1, starting transfers between devices, body(): input_grad = lax.all_to_all(total, 'z', 0, 0, tiled=True).sum(axis=0)  7.64 us
    all_to_all x1, blocking collectives, body(): total = lax.all_to_all(total, 'core', 0, 0, tiled=True).sum(axis=0)  4.58 us
  transfers between devices with their start and end apart: 1, of which 1 were waited for; matrix products, arithmetic and copies ran while one was open for 3% of the time, Pallas kernels for 0%

profile of v2, /device:TPU:32, one launch (start us, length us, event | category | flops | bytes accessed | tf_op | source)
XLA Modules:
  0.0 190.0 jit_solution(16453941029536034708)
XLA Ops:
  0.6 0.0 copy-start
  0.6 0.0 copy-start.3
  0.7 35.9 %all_gather.6 = bf16[512,512]{1,0:T(8,128)(2,1)S(1)} all-gather(bf16[16,512]{1,0:T(8,128)(2,1)} %param.5), channel_id=1, replica_groups=mesh['z'=16,'core'=2,'col'=16] {'z','core'}, dimensions={0}, use_global_device_ids=true | all-gather | bytes 540672 | tf_op jit(solution)/shard_map/all_gather | solution.py:22
  36.5 30.6 %all_gather.7 = bf16[512,512]{1,0:T(8,128)(2,1)S(1)} all-gather(bf16[16,512]{1,0:T(8,128)(2,1)} %param.6), channel_id=1, replica_groups=mesh['z'=16,'core'=2,'col'=16] {'z','core'}, dimensions={0}, use_global_device_ids=true | all-gather | bytes 540672 | tf_op jit(solution)/shard_map/all_gather | solution.py:23
  67.2 1.5 fusion.5
  68.7 0.0 copy-done
  68.7 0.4 fusion.4
  69.1 0.0 copy-done.3
  69.1 0.5 fusion.6
  69.6 0.5 pad_maximum_fusion
  70.1 47.1 %all_to_all.20 = f32[3,16,32,512]{3,2,0,1:T(8,128)} all-to-all(f32[3,16,32,512]{3,2,0,1:T(8,128)S(1)} %pad_maximum_fusion), channel_id=1, replica_groups=mesh['z'=16,'core'=2,'col'=16] {'col'}, dimensions={1} | all-to-all | bytes 6291456 | tf_op jit(solution)/shard_map/all_to_all | solution.py:35
  117.2 2.2 %reduce_sum.27 = f32[3,32,512]{2,1,0:T(8,128)S(1)} reduce(f32[3,16,32,512]{3,2,0,1:T(8,128)} %all_to_all.20, f32[]{:T(128)} %constant.0.clone.1), dimensions={1}, to_apply=%region_0.0 | reduce | flops 737280 | bytes 3342340 | tf_op jit(solution)/shard_map/reduce_sum | solution.py:36
  119.5 0.2 broadcast_in_dim.2
  119.7 25.2 %all_to_all.21 = bf16[16,3,32,512]{3,2,1,0:T(8,128)(2,1)S(1)} all-to-all(bf16[16,3,32,512]{3,2,1,0:T(8,128)(2,1)S(1)} %broadcast_in_dim.2), channel_id=1, replica_groups=mesh['z'=16,'core'=2,'col'=16] {'col'}, dimensions={0} | all-to-all | bytes 3145728 | tf_op jit(solution)/shard_map/all_to_all | solution.py:39
  144.9 0.0 copy-start.1
  144.9 0.9 fusion.3
  145.8 0.0 copy-start.2
  145.8 0.5 fusion.7
  146.2 0.0 copy-done.1
  146.3 0.5 convolution_add_fusion
  146.7 0.1 copy.24
  146.8 0.0 copy-done.2
  146.8 4.6 %all_to_all.22 = f32[2,16,16,512]{3,2,1,0:T(8,128)S(1)} all-to-all(f32[2,16,16,512]{3,2,1,0:T(8,128)S(1)} %bitcast.39), channel_id=1, replica_groups=mesh['z'=16,'core'=2,'col'=16] {'core'}, dimensions={0} | all-to-all | bytes 2097152 | tf_op jit(solution)/shard_map/all_to_all | solution.py:56
  151.4 0.9 reduce_sum.28
  152.3 7.6 %all-to-all-start.3 = ((f32[16,16,512]{2,1,0:T(8,128)}), f32[16,16,512]{2,1,0:T(8,128)S(1)}, u32[]{:S(2)}, u32[]{:S(2)}) async-start(f32[16,16,512]{2,1,0:T(8,128)} %reduce_sum.28), calls=%async_computation.3 | async-start | bytes 1048576 | tf_op jit(solution)/shard_map/all_to_all | solution.py:57
  160.0 1.5 fusion
  161.5 1.0 copy.21
  162.5 0.5 fusion.1
  163.0 1.0 copy.22
  164.0 2.3 %convolution_convert_fusion = bf16[512,512]{1,0:T(8,128)(2,1)} fusion(bf16[512,512]{1,0:T(8,128)(2,1)} %bitcast.47, bf16[512,512]{1,0:T(8,128)(2,1)S(1)} %all_gather.7), kind=kOutput, calls=%fused_computation.2 | convolution fusion | flops 268697600 | bytes 1572864 | tf_op jit(solution)/shard_map/dot_general | solution.py:48
  166.3 23.1 %all-to-all-done.3 = f32[16,16,512]{2,1,0:T(8,128)S(1)} async-done(((f32[16,16,512]{2,1,0:T(8,128)}), f32[16,16,512]{2,1,0:T(8,128)S(1)}, u32[]{:S(2)}, u32[]{:S(2)}) %all-to-all-start.3) | async-done | bytes 524320 | tf_op jit(solution)/shard_map/all_to_all | solution.py:57
  189.4 0.6 reduce_sum.29
  (2 shorter events, 0.1 us)
Async XLA Ops:
  0.6 68.0 %copy-start = (bf16[512,512]{1,0:T(8,128)(2,1)S(1)}, bf16[512,512]{1,0:T(8,128)(2,1)}, u32[]{:S(2)}) copy-start(bf16[512,512]{1,0:T(8,128)(2,1)} %param.7) | copy-start | bytes 1572868
  0.6 68.5 %copy-start.3 = (bf16[512,512]{1,0:T(8,128)(2,1)S(1)}, bf16[512,512]{1,0:T(8,128)(2,1)}, u32[]{:S(2)}) copy-start(bf16[512,512]{1,0:T(8,128)(2,1)} %param.9) | copy-start | bytes 1572868
  144.9 1.4 copy-start.1
  145.8 1.1 copy-start.2
  152.3 37.0 %all-to-all-start.3 = ((f32[16,16,512]{2,1,0:T(8,128)}), f32[16,16,512]{2,1,0:T(8,128)S(1)}, u32[]{:S(2)}, u32[]{:S(2)}) async-start(f32[16,16,512]{2,1,0:T(8,128)} %reduce_sum.28), calls=%async_computation.3 | async-start | bytes 1048576 | tf_op jit(solution)/shard_map/all_to_all | solution.py:57

commit v3 on v2

--- a/solution.py
+++ b/solution.py
@@ -15,12 +15,25 @@
     return (hidden, gate_grad, up_grad)
 
 
+def gather_rows(tokens, out_grad, n_z, n_core):
+    both = jnp.stack([tokens, out_grad])
+    both = jnp.broadcast_to(both[None], (n_core,) + both.shape)
+    both = lax.all_to_all(both, "core", 0, 0, tiled=True)
+    mine = lax.dynamic_index_in_dim(both, lax.axis_index("core"), axis=1, keepdims=False)
+    mine = mine.reshape((1,) + (-1,) + mine.shape[2:])
+    mine = jnp.broadcast_to(mine, (n_z,) + mine.shape[1:])
+    mine = lax.all_to_all(mine, "z", 0, 0, tiled=True)
+    mine = mine.reshape((1, -1) + mine.shape[2:])
+    mine = jnp.broadcast_to(mine, (n_core,) + mine.shape[1:])
+    full = lax.all_to_all(mine, "core", 0, 0, tiled=True)
+    return full[0], full[1]
+
+
 def body(tokens, out_grad, gate_weight, up_weight, down_weight):
     n_col = lax.psum(1, "col")
     n_z = lax.psum(1, "z")
     n_core = lax.psum(1, "core")
-    rows_all = lax.all_gather(tokens, ROW, axis=0, tiled=True)
-    grads_all = lax.all_gather(out_grad, ROW, axis=0, tiled=True)
+    rows_all, grads_all = gather_rows(tokens, out_grad, n_z, n_core)
     n_tok, width = rows_all.shape
     contract_cols = (((1,), (1,)), ((), ()))
     contract_rows = (((0,), (0,)), ((), ()))

time: 191 us -> 178 us (0.932)
  blocking collectives: 143 us -> 126 us
  waiting for transfers between devices: 23.1 us -> 26 us
  starting transfers between devices: 7.64 us -> 9.67 us
    all_gather x2 -> x0, blocking collectives: 66.5 us -> none  [the longest x1 35.9 us: body(): rows_all = lax.all_gather(tokens, ROW, axis=0, tiled=True)]
    all_to_all x0 -> x2, blocking collectives: none -> 49.2 us  [the longest x1 44.5 us: gather_rows(): mine = lax.all_to_all(mine, 'z', 0, 0, tiled=True)]
    all_to_all x0 -> x1, starting transfers between devices: none -> 3.3 us  [gather_rows(): both = lax.all_to_all(both, 'core', 0, 0, tiled=True)]
    unnamed x10, local copies, waits for them, and re-layouts: 2.03 us -> 0.1 us
  transfers between devices with their start and end apart: 1 -> 2, of which waited for: 1 -> 2; matrix products, arithmetic and copies ran while one was open for 3% -> 3% of each run, Pallas kernels for 0% -> 0%
where the time goes in v3:
time: 178 us; the launch traced here: 177 us
  blocking collectives  126 us (71%)
  waiting for transfers between devices  26 us (15%)
  starting transfers between devices  9.67 us (5%)
  matrix products  7.07 us (4%)
  other arithmetic  5.13 us (3%)
  local copies, waits for them, and re-layouts  2.63 us (1%)
    all_to_all x1, blocking collectives, body(): parts = lax.all_to_all(parts, 'col', 1, 1, tiled=True)  46.9 us
    all_to_all x1, blocking collectives, gather_rows(): mine = lax.all_to_all(mine, 'z', 0, 0, tiled=True)  44.5 us
    all_to_all x1, blocking collectives, body(): spread = lax.all_to_all(spread, 'col', 0, 0, tiled=True)  25.2 us
    all_to_all x1, waiting for transfers between devices, body(): input_grad = lax.all_to_all(total, 'z', 0, 0, tiled=True).sum(axis=0)  24.6 us
    all_to_all x1, starting transfers between devices, body(): input_grad = lax.all_to_all(total, 'z', 0, 0, tiled=True).sum(axis=0)  6.37 us
    all_to_all x1, blocking collectives, gather_rows(): full = lax.all_to_all(mine, 'core', 0, 0, tiled=True)  4.71 us
    all_to_all x1, blocking collectives, body(): total = lax.all_to_all(total, 'core', 0, 0, tiled=True).sum(axis=0)  4.58 us
  transfers between devices with their start and end apart: 2, of which 2 were waited for; matrix products, arithmetic and copies ran while one was open for 3% of the time, Pallas kernels for 0%

profile of v3, /device:TPU:32, one launch (start us, length us, event | category | flops | bytes accessed | tf_op | source)
XLA Modules:
  0.0 177.1 jit_solution(5265312377821003721)
XLA Ops:
  0.6 0.0 copy-start
  0.6 0.8 pad_maximum_fusion.2
  1.4 0.6 broadcast_in_dim.12
  2.1 3.3 %all-to-all-start = ((bf16[2,2,16,512]{3,2,1,0:T(8,128)(2,1)}), bf16[2,2,16,512]{3,2,1,0:T(8,128)(2,1)S(1)}, u32[]{:S(2)}, u32[]{:S(2)}) async-start(bf16[2,2,16,512]{3,2,1,0:T(8,128)(2,1)} %broadcast_in_dim.12), calls=%async_computation | async-start | bytes 131072 | tf_op jit(solution)/shard_map/all_to_all | solution.py:21
  5.4 1.4 all-to-all-done
  6.8 44.5 %all_to_all.35 = bf16[16,32,512]{2,1,0:T(8,128)(2,1)S(1)} all-to-all(bf16[16,32,512]{2,1,0:T(8,128)(2,1)S(1)} %broadcast_in_dim.28), channel_id=1, replica_groups=mesh['z'=16,'core'=2,'col'=16] {'z'}, dimensions={0} | all-to-all | bytes 1048576 | tf_op jit(solution)/shard_map/all_to_all | solution.py:25
  51.3 0.0 copy-start.1
  51.3 0.1 broadcast_in_dim.30
  51.4 4.7 %all_to_all.36 = bf16[2,512,512]{2,1,0:T(8,128)(2,1)S(1)} all-to-all(bf16[2,512,512]{2,1,0:T(8,128)(2,1)S(1)} %broadcast_in_dim.30), channel_id=1, replica_groups=mesh['z'=16,'core'=2,'col'=16] {'core'}, dimensions={0} | all-to-all | bytes 2097152 | tf_op jit(solution)/shard_map/all_to_all | solution.py:28
  56.1 0.0 copy-start.3
  56.1 0.1 fusion.11
  56.2 0.0 copy-done.1
  56.2 0.4 convolution_bitcast_fusion.1
  56.6 0.0 copy-done
  56.6 0.4 convolution_bitcast_fusion.2
  57.1 0.1 copy-done.3
  57.2 0.5 convolution_bitcast_fusion
  57.6 0.5 pad_maximum_fusion
  58.2 0.5 copy.11
  58.7 46.9 %all_to_all.37 = f32[3,16,32,512]{3,2,0,1:T(8,128)} all-to-all(f32[3,16,32,512]{3,2,0,1:T(8,128)S(1)} %copy.11), channel_id=1, replica_groups=mesh['z'=16,'core'=2,'col'=16] {'col'}, dimensions={1} | all-to-all | bytes 6291456 | tf_op jit(solution)/shard_map/all_to_all | solution.py:48
  105.6 2.2 %reduce_sum.27 = f32[3,32,512]{2,1,0:T(8,128)S(1)} reduce(f32[3,16,32,512]{3,2,0,1:T(8,128)} %all_to_all.37, f32[]{:T(128)} %constant.14.clone.1), dimensions={1}, to_apply=%region_0.1 | reduce | flops 737280 | bytes 3342340 | tf_op jit(solution)/shard_map/reduce_sum | solution.py:49
  107.9 0.2 broadcast_in_dim.31
  108.0 25.2 %all_to_all.38 = bf16[16,3,32,512]{3,2,1,0:T(8,128)(2,1)S(1)} all-to-all(bf16[16,3,32,512]{3,2,1,0:T(8,128)(2,1)S(1)} %broadcast_in_dim.31), channel_id=1, replica_groups=mesh['z'=16,'core'=2,'col'=16] {'col'}, dimensions={0} | all-to-all | bytes 3145728 | tf_op jit(solution)/shard_map/all_to_all | solution.py:52
  133.3 0.9 fusion.10
  134.2 0.0 copy-start.2
  134.2 0.5 fusion.12
  134.6 0.5 convolution_add_fusion
  135.1 0.1 copy.14
  135.2 0.0 copy-done.2
  135.2 4.6 %all_to_all.39 = f32[2,16,16,512]{3,2,1,0:T(8,128)S(1)} all-to-all(f32[2,16,16,512]{3,2,1,0:T(8,128)S(1)} %bitcast.51), channel_id=1, replica_groups=mesh['z'=16,'core'=2,'col'=16] {'core'}, dimensions={0} | all-to-all | bytes 2097152 | tf_op jit(solution)/shard_map/all_to_all | solution.py:69
  139.8 0.9 reduce_sum.28
  140.7 0.0 copy-start.4
  140.7 6.4 %all-to-all-start.6 = ((f32[16,16,512]{2,1,0:T(8,128)}), f32[16,16,512]{2,1,0:T(8,128)S(1)}, u32[]{:S(2)}, u32[]{:S(2)}) async-start(f32[16,16,512]{2,1,0:T(8,128)} %reduce_sum.28), calls=%async_computation.6 | async-start | bytes 1048576 | tf_op jit(solution)/shard_map/all_to_all | solution.py:70
  147.1 2.3 %convolution_convert_fusion.1 = bf16[512,512]{1,0:T(8,128)(2,1)} fusion(bf16[512,512]{1,0:T(8,128)(2,1)} %bitcast.56, bf16[2,512,512]{2,1,0:T(8,128)(2,1)S(1)} %all_to_all.36), kind=kOutput, calls=%fused_computation.6 | convolution fusion | flops 268697600 | bytes 1572864 | tf_op jit(solution)/shard_map/dot_general | solution.py:58
  149.4 1.3 convolution_convert_fusion.2
  150.6 0.0 copy-done.4
  150.6 1.3 convolution_convert_fusion
  151.9 24.6 %all-to-all-done.6 = f32[16,16,512]{2,1,0:T(8,128)S(1)} async-done(((f32[16,16,512]{2,1,0:T(8,128)}), f32[16,16,512]{2,1,0:T(8,128)S(1)}, u32[]{:S(2)}, u32[]{:S(2)}) %all-to-all-start.6) | async-done | bytes 524320 | tf_op jit(solution)/shard_map/all_to_all | solution.py:70
  176.5 0.6 reduce_sum.29
  (4 shorter events, 0.1 us)
Async XLA Ops:
  0.6 56.0 %copy-start = (bf16[512,512]{1,0:T(8,128)(2,1)S(1)}, bf16[512,512]{1,0:T(8,128)(2,1)}, u32[]{:S(2)}) copy-start(bf16[512,512]{1,0:T(8,128)(2,1)} %param.7) | copy-start | bytes 1572868
  2.1 4.7 %all-to-all-start = ((bf16[2,2,16,512]{3,2,1,0:T(8,128)(2,1)}), bf16[2,2,16,512]{3,2,1,0:T(8,128)(2,1)S(1)}, u32[]{:S(2)}, u32[]{:S(2)}) async-start(bf16[2,2,16,512]{3,2,1,0:T(8,128)(2,1)} %broadcast_in_dim.12), calls=%async_computation | async-start | bytes 131072 | tf_op jit(solution)/shard_map/all_to_all | solution.py:21
  51.3 4.9 %copy-start.1 = (bf16[512,512]{1,0:T(8,128)(2,1)S(1)}, bf16[512,512]{1,0:T(8,128)(2,1)}, u32[]{:S(2)}) copy-start(bf16[512,512]{1,0:T(8,128)(2,1)} %param.8) | copy-start | bytes 1572868
  56.1 1.0 copy-start.3
  134.2 1.1 copy-start.2
  140.7 9.9 %copy-start.4 = (bf16[1,16,32,512]{3,2,0,1:T(8,128)(2,1)S(1)}, bf16[1,16,32,512]{3,2,0,1:T(8,128)(2,1)}, u32[]{:S(2)}) copy-start(bf16[1,16,32,512]{3,2,0,1:T(8,128)(2,1)} %get-tuple-element.4) | copy-start | bytes 1572868
  140.7 35.8 %all-to-all-start.6 = ((f32[16,16,512]{2,1,0:T(8,128)}), f32[16,16,512]{2,1,0:T(8,128)S(1)}, u32[]{:S(2)}, u32[]{:S(2)}) async-start(f32[16,16,512]{2,1,0:T(8,128)} %reduce_sum.28), calls=%async_computation.6 | async-start | bytes 1048576 | tf_op jit(solution)/shard_map/all_to_all | solution.py:70

commit v4 on v3

--- a/solution.py
+++ b/solution.py
@@ -17,13 +17,10 @@
 
 def gather_rows(tokens, out_grad, n_z, n_core):
     both = jnp.stack([tokens, out_grad])
-    both = jnp.broadcast_to(both[None], (n_core,) + both.shape)
-    both = lax.all_to_all(both, "core", 0, 0, tiled=True)
-    mine = lax.dynamic_index_in_dim(both, lax.axis_index("core"), axis=1, keepdims=False)
-    mine = mine.reshape((1,) + (-1,) + mine.shape[2:])
-    mine = jnp.broadcast_to(mine, (n_z,) + mine.shape[1:])
-    mine = lax.all_to_all(mine, "z", 0, 0, tiled=True)
-    mine = mine.reshape((1, -1) + mine.shape[2:])
+    both = jnp.broadcast_to(both[None], (n_z,) + both.shape)
+    both = both.reshape((n_z * n_core,) + tokens.shape)
+    mine = lax.all_to_all(both, ROW, 0, 0, tiled=True)
+    mine = mine.reshape((1, -1) + tokens.shape[1:])
     mine = jnp.broadcast_to(mine, (n_core,) + mine.shape[1:])
     full = lax.all_to_all(mine, "core", 0, 0, tiled=True)
     return full[0], full[1]

time: 178 us -> 175 us (0.983)
  starting transfers between devices: 9.67 us -> 5.33 us
  blocking collectives: 126 us -> 129 us
    all_to_all x1 -> x0, starting transfers between devices: 3.3 us -> none  [gather_rows(): both = lax.all_to_all(both, 'core', 0, 0, tiled=True)]
    all_to_all x1, blocking collectives: 44.5 us -> 47.3 us  [gather_rows(): mine = lax.all_to_all(both, ROW, 0, 0, tiled=True)]
  transfers between devices with their start and end apart: 2 -> 1, of which waited for: 2 -> 1; matrix products, arithmetic and copies ran while one was open for 3% -> 3% of each run, Pallas kernels for 0% -> 0%
where the time goes in v4:
time: 175 us; the launch traced here: 174 us
  blocking collectives  129 us (74%)
  waiting for transfers between devices  25.2 us (14%)
  matrix products  7.07 us (4%)
  starting transfers between devices  5.33 us (3%)
  other arithmetic  5.12 us (3%)
  local copies, waits for them, and re-layouts  1.99 us (1%)
    all_to_all x1, blocking collectives, gather_rows(): mine = lax.all_to_all(both, ROW, 0, 0, tiled=True)  47.3 us
    all_to_all x1, blocking collectives, body(): parts = lax.all_to_all(parts, 'col', 1, 1, tiled=True)  46.9 us
    all_to_all x1, blocking collectives, body(): spread = lax.all_to_all(spread, 'col', 0, 0, tiled=True)  25.2 us
    all_to_all x1, waiting for transfers between devices, body(): input_grad = lax.all_to_all(total, 'z', 0, 0, tiled=True).sum(axis=0)  25.2 us
    all_to_all x1, starting transfers between devices, body(): input_grad = lax.all_to_all(total, 'z', 0, 0, tiled=True).sum(axis=0)  5.33 us
    all_to_all x1, blocking collectives, gather_rows(): full = lax.all_to_all(mine, 'core', 0, 0, tiled=True)  4.71 us
    all_to_all x1, blocking collectives, body(): total = lax.all_to_all(total, 'core', 0, 0, tiled=True).sum(axis=0)  4.58 us
  transfers between devices with their start and end apart: 1, of which 1 were waited for; matrix products, arithmetic and copies ran while one was open for 3% of the time, Pallas kernels for 0%

profile of v4, /device:TPU:32, one launch (start us, length us, event | category | flops | bytes accessed | tf_op | source)
XLA Modules:
  0.0 174.2 jit_solution(14972271620776225612)
XLA Ops:
  0.6 0.0 copy-start
  0.6 0.8 pad_maximum_fusion.2
  1.4 0.1 broadcast_in_dim.8
  1.5 47.3 %all_to_all.30 = bf16[32,16,512]{2,1,0:T(8,128)(2,1)S(1)} all-to-all(bf16[32,16,512]{2,1,0:T(8,128)(2,1)S(1)} %bitcast.53), channel_id=1, replica_groups=mesh['z'=16,'core'=2,'col'=16] {'z','core'}, dimensions={0} | all-to-all | bytes 1048576 | tf_op jit(solution)/shard_map/all_to_all | solution.py:22
  48.8 0.0 copy-start.1
  48.8 0.1 broadcast_in_dim.10
  48.9 4.7 %all_to_all.31 = bf16[2,512,512]{2,1,0:T(8,128)(2,1)S(1)} all-to-all(bf16[2,512,512]{2,1,0:T(8,128)(2,1)S(1)} %broadcast_in_dim.10), channel_id=1, replica_groups=mesh['z'=16,'core'=2,'col'=16] {'core'}, dimensions={0} | all-to-all | bytes 2097152 | tf_op jit(solution)/shard_map/all_to_all | solution.py:25
  53.6 0.0 copy-start.3
  53.6 0.1 fusion.11
  53.7 0.0 copy-done.1
  53.7 0.4 convolution_bitcast_fusion.1
  54.1 0.0 copy-done
  54.2 0.4 convolution_bitcast_fusion.2
  54.6 0.1 copy-done.3
  54.7 0.5 convolution_bitcast_fusion
  55.1 0.5 pad_maximum_fusion
  55.7 0.5 copy.11
  56.2 46.9 %all_to_all.32 = f32[3,16,32,512]{3,2,0,1:T(8,128)} all-to-all(f32[3,16,32,512]{3,2,0,1:T(8,128)S(1)} %copy.11), channel_id=1, replica_groups=mesh['z'=16,'core'=2,'col'=16] {'col'}, dimensions={1} | all-to-all | bytes 6291456 | tf_op jit(solution)/shard_map/all_to_all | solution.py:45
  103.1 2.2 %reduce_sum.27 = f32[3,32,512]{2,1,0:T(8,128)S(1)} reduce(f32[3,16,32,512]{3,2,0,1:T(8,128)} %all_to_all.32, f32[]{:T(128)} %constant.0.clone.1), dimensions={1}, to_apply=%region_0.0 | reduce | flops 737280 | bytes 3342340 | tf_op jit(solution)/shard_map/reduce_sum | solution.py:46
  105.4 0.2 broadcast_in_dim.22
  105.5 25.2 %all_to_all.33 = bf16[16,3,32,512]{3,2,1,0:T(8,128)(2,1)S(1)} all-to-all(bf16[16,3,32,512]{3,2,1,0:T(8,128)(2,1)S(1)} %broadcast_in_dim.22), channel_id=1, replica_groups=mesh['z'=16,'core'=2,'col'=16] {'col'}, dimensions={0} | all-to-all | bytes 3145728 | tf_op jit(solution)/shard_map/all_to_all | solution.py:49
  130.8 0.9 fusion.10
  131.7 0.0 copy-start.2
  131.7 0.5 fusion.12
  132.1 0.5 convolution_add_fusion
  132.6 0.1 copy.14
  132.7 0.0 copy-done.2
  132.7 4.6 %all_to_all.34 = f32[2,16,16,512]{3,2,1,0:T(8,128)S(1)} all-to-all(f32[2,16,16,512]{3,2,1,0:T(8,128)S(1)} %bitcast.51), channel_id=1, replica_groups=mesh['z'=16,'core'=2,'col'=16] {'core'}, dimensions={0} | all-to-all | bytes 2097152 | tf_op jit(solution)/shard_map/all_to_all | solution.py:66
  137.3 0.9 reduce_sum.28
  138.2 0.0 copy-start.4
  138.2 5.3 %all-to-all-start.5 = ((f32[16,16,512]{2,1,0:T(8,128)}), f32[16,16,512]{2,1,0:T(8,128)S(1)}, u32[]{:S(2)}, u32[]{:S(2)}) async-start(f32[16,16,512]{2,1,0:T(8,128)} %reduce_sum.28), calls=%async_computation.5 | async-start | bytes 1048576 | tf_op jit(solution)/shard_map/all_to_all | solution.py:67
  143.5 2.3 %convolution_convert_fusion.1 = bf16[512,512]{1,0:T(8,128)(2,1)} fusion(bf16[512,512]{1,0:T(8,128)(2,1)} %bitcast.57, bf16[2,512,512]{2,1,0:T(8,128)(2,1)S(1)} %all_to_all.31), kind=kOutput, calls=%fused_computation.6 | convolution fusion | flops 268697600 | bytes 1572864 | tf_op jit(solution)/shard_map/dot_general | solution.py:55
  145.8 1.3 convolution_convert_fusion.2
  147.1 0.0 copy-done.4
  147.1 1.3 convolution_convert_fusion
  148.3 25.2 %all-to-all-done.5 = f32[16,16,512]{2,1,0:T(8,128)S(1)} async-done(((f32[16,16,512]{2,1,0:T(8,128)}), f32[16,16,512]{2,1,0:T(8,128)S(1)}, u32[]{:S(2)}, u32[]{:S(2)}) %all-to-all-start.5) | async-done | bytes 524320 | tf_op jit(solution)/shard_map/all_to_all | solution.py:67
  173.5 0.6 reduce_sum.29
  (2 shorter events, 0.1 us)
Async XLA Ops:
  0.6 53.5 %copy-start = (bf16[512,512]{1,0:T(8,128)(2,1)S(1)}, bf16[512,512]{1,0:T(8,128)(2,1)}, u32[]{:S(2)}) copy-start(bf16[512,512]{1,0:T(8,128)(2,1)} %param.7) | copy-start | bytes 1572868
  48.8 4.9 %copy-start.1 = (bf16[512,512]{1,0:T(8,128)(2,1)S(1)}, bf16[512,512]{1,0:T(8,128)(2,1)}, u32[]{:S(2)}) copy-start(bf16[512,512]{1,0:T(8,128)(2,1)} %param.8) | copy-start | bytes 1572868
  53.6 1.0 copy-start.3
  131.7 1.1 copy-start.2
  138.2 8.9 %copy-start.4 = (bf16[1,16,32,512]{3,2,0,1:T(8,128)(2,1)S(1)}, bf16[1,16,32,512]{3,2,0,1:T(8,128)(2,1)}, u32[]{:S(2)}) copy-start(bf16[1,16,32,512]{3,2,0,1:T(8,128)(2,1)} %get-tuple-element.4) | copy-start | bytes 1572868
  138.2 35.3 %all-to-all-start.5 = ((f32[16,16,512]{2,1,0:T(8,128)}), f32[16,16,512]{2,1,0:T(8,128)S(1)}, u32[]{:S(2)}, u32[]{:S(2)}) async-start(f32[16,16,512]{2,1,0:T(8,128)} %reduce_sum.28), calls=%async_computation.5 | async-start | bytes 1048576 | tf_op jit(solution)/shard_map/all_to_all | solution.py:67

commit v5 on v4

--- a/solution.py
+++ b/solution.py
@@ -41,14 +41,14 @@
     )
     hid = gate_part.shape[1]
     chunk = n_tok // n_col
-    parts = jnp.stack([gate_part, up_part, grad_part]).reshape(3, n_col, chunk, hid)
-    parts = lax.all_to_all(parts, "col", 1, 1, tiled=True)
-    gate, up, hidden_grad = parts.sum(axis=1)
-    small = jnp.stack(pointwise(gate, up, hidden_grad))
+    parts = jnp.concatenate([gate_part, up_part, grad_part], axis=1)
+    parts = lax.all_to_all(parts.reshape(n_col, chunk, 3 * hid), "col", 0, 0, tiled=True)
+    parts = parts.sum(axis=0)
+    gate, up, hidden_grad = parts[:, :hid], parts[:, hid:2 * hid], parts[:, 2 * hid:]
+    small = jnp.concatenate(pointwise(gate, up, hidden_grad), axis=1)
     spread = jnp.broadcast_to(small[None], (n_col,) + small.shape)
-    spread = lax.all_to_all(spread, "col", 0, 0, tiled=True)
-    spread = spread.transpose(1, 0, 2, 3).reshape(3, n_tok, hid)
-    hidden, gate_grad, up_grad = spread[0], spread[1], spread[2]
+    spread = lax.all_to_all(spread, "col", 0, 0, tiled=True).reshape(n_tok, 3 * hid)
+    hidden, gate_grad, up_grad = spread[:, :hid], spread[:, hid:2 * hid], spread[:, 2 * hid:]
     gate_weight_grad = lax.dot_general(
         rows_all, gate_grad, contract_rows, preferred_element_type=jnp.float32
     ).astype(jnp.bfloat16)

time: 175 us -> 183 us (1.046)
  other arithmetic: 5.12 us -> 8.79 us
  local copies, waits for them, and re-layouts: 1.99 us -> 4.5 us
    concatenate x0 -> x1, local copies, waits for them, and re-layouts: none -> 3.55 us  [body(): parts = jnp.concatenate([gate_part, up_part, grad_part], axis=1)]
    concatenate x0 -> x2, other arithmetic: none -> 2.02 us  [the longest x1 2.01 us: body(): parts = jnp.concatenate([gate_part, up_part, grad_part], axis=1)]
  transfers between devices with their start and end apart: 1 -> 1, of which waited for: 1 -> 1; matrix products, arithmetic and copies ran while one was open for 3% -> 2% of each run, Pallas kernels for 0% -> 0%
where the time goes in v5:
time: 183 us; the launch traced here: 182 us
  blocking collectives  130 us (71%)
  waiting for transfers between devices  26.3 us (14%)
  other arithmetic  8.79 us (5%)
  matrix products  6.11 us (3%)
  starting transfers between devices  5.8 us (3%)
  local copies, waits for them, and re-layouts  4.5 us (2%)
    all_to_all x1, blocking collectives, gather_rows(): mine = lax.all_to_all(both, ROW, 0, 0, tiled=True)  47.3 us
    all_to_all x1, blocking collectives, body(): lax.all_to_all(parts.reshape(n_col, chunk, 3 * hid), 'col', 0, 0, tiled=T...  47.1 us
    all_to_all x1, waiting for transfers between devices, body(): input_grad = lax.all_to_all(total, 'z', 0, 0, tiled=True).sum(axis=0)  26.3 us
    all_to_all x1, blocking collectives, body(): lax.all_to_all(spread, 'col', 0, 0, tiled=True).reshape(n_tok, 3 * hid)  25.2 us
    all_to_all x1, starting transfers between devices, body(): input_grad = lax.all_to_all(total, 'z', 0, 0, tiled=True).sum(axis=0)  5.8 us
    all_to_all x1, blocking collectives, body(): total = lax.all_to_all(total, 'core', 0, 0, tiled=True).sum(axis=0)  5.36 us
    all_to_all x1, blocking collectives, gather_rows(): full = lax.all_to_all(mine, 'core', 0, 0, tiled=True)  4.71 us
  transfers between devices with their start and end apart: 1, of which 1 were waited for; matrix products, arithmetic and copies ran while one was open for 2% of the time, Pallas kernels for 0%

profile of v5, /device:TPU:32, one launch (start us, length us, event | category | flops | bytes accessed | tf_op | source)
XLA Modules:
  0.0 182.0 jit_solution(7497968674131641834)
XLA Ops:
  0.6 0.0 copy-start
  0.6 0.8 pad_maximum_fusion.2
  1.4 0.1 broadcast_in_dim.8
  1.5 47.3 %all_to_all.30 = bf16[32,16,512]{2,1,0:T(8,128)(2,1)S(1)} all-to-all(bf16[32,16,512]{2,1,0:T(8,128)(2,1)S(1)} %bitcast.34), channel_id=1, replica_groups=mesh['z'=16,'core'=2,'col'=16] {'z','core'}, dimensions={0} | all-to-all | bytes 1048576 | tf_op jit(solution)/shard_map/all_to_all | solution.py:22
  48.8 0.0 copy-start.1
  48.8 0.1 broadcast_in_dim.10
  48.9 0.0 copy-start.3
  48.9 4.7 %all_to_all.31 = bf16[2,512,512]{2,1,0:T(8,128)(2,1)S(1)} all-to-all(bf16[2,512,512]{2,1,0:T(8,128)(2,1)S(1)} %broadcast_in_dim.10), channel_id=1, replica_groups=mesh['z'=16,'core'=2,'col'=16] {'core'}, dimensions={0} | all-to-all | bytes 2097152 | tf_op jit(solution)/shard_map/all_to_all | solution.py:25
  53.6 0.0 copy-done.1
  53.6 0.5 fusion.7
  54.1 0.0 copy-done.3
  54.1 0.5 fusion.1
  54.6 0.0 copy-done
  54.6 0.5 fusion.8
  55.1 2.0 %pad_maximum_fusion = f32[512,1536]{0,1:T(8,128)} fusion(f32[512,512]{0,1:T(8,128)S(1)} %fusion.1, f32[512,512]{0,1:T(8,128)S(1)} %fusion.7, f32[512,512]{0,1:T(8,128)S(1)} %fusion.8), kind=kLoop, calls=%fused_computation | loop fusion | flops 1572864 | bytes 6291456 | tf_op jit(solution)/shard_map/concatenate | solution.py:44
  57.1 3.5 %copy.12 = f32[512,1536]{1,0:T(8,128)} copy(f32[512,1536]{0,1:T(8,128)} %pad_maximum_fusion) | data formatting | bytes 6291456 | tf_op jit(solution)/shard_map/concatenate | solution.py:44
  60.7 47.1 %all_to_all.32 = f32[16,32,1536]{2,1,0:T(8,128)} all-to-all(f32[16,32,1536]{2,1,0:T(8,128)} %bitcast.25), channel_id=1, replica_groups=mesh['z'=16,'core'=2,'col'=16] {'col'}, dimensions={0} | all-to-all | bytes 6291456 | tf_op jit(solution)/shard_map/all_to_all | solution.py:45
  107.7 2.1 %reduce_sum.27 = f32[32,1536]{1,0:T(8,128)S(1)} reduce(f32[16,32,1536]{2,1,0:T(8,128)} %all_to_all.32, f32[]{:T(128)} %constant.0.clone.1), dimensions={0}, to_apply=%region_0.0 | reduce | flops 737280 | bytes 3342340 | tf_op jit(solution)/shard_map/reduce_sum | solution.py:46
  109.9 0.1 broadcast_in_dim.22
  110.0 25.2 %all_to_all.33 = bf16[16,32,1536]{2,1,0:T(8,128)(2,1)S(1)} all-to-all(bf16[16,32,1536]{2,1,0:T(8,128)(2,1)S(1)} %broadcast_in_dim.22), channel_id=1, replica_groups=mesh['z'=16,'core'=2,'col'=16] {'col'}, dimensions={0} | all-to-all | bytes 3145728 | tf_op jit(solution)/shard_map/all_to_all | solution.py:50
  135.2 0.0 copy-start.2
  135.2 0.5 fusion.5
  135.7 0.6 copy-done.2
  136.3 0.5 convolution_add_fusion
  136.8 0.1 copy.15
  136.9 5.4 %all_to_all.34 = f32[2,16,16,512]{3,2,1,0:T(8,128)} all-to-all(f32[2,16,16,512]{3,2,1,0:T(8,128)S(1)} %bitcast.32), channel_id=1, replica_groups=mesh['z'=16,'core'=2,'col'=16] {'core'}, dimensions={0} | all-to-all | bytes 2097152 | tf_op jit(solution)/shard_map/all_to_all | solution.py:66
  142.2 2.2 %reduce_sum.28 = f32[16,16,512]{2,1,0:T(8,128)} reduce(f32[2,16,16,512]{3,2,1,0:T(8,128)} %all_to_all.34, f32[]{:T(128)} %constant.0.clone.1), dimensions={0}, to_apply=%region_1.0 | reduce | flops 131072 | bytes 1572868 | tf_op jit(solution)/shard_map/reduce_sum | solution.py:66
  144.4 5.8 %all-to-all-start.5 = ((f32[16,16,512]{2,1,0:T(8,128)}), f32[16,16,512]{2,1,0:T(8,128)}, u32[]{:S(2)}, u32[]{:S(2)}) async-start(f32[16,16,512]{2,1,0:T(8,128)} %reduce_sum.28), calls=%async_computation.5 | async-start | bytes 1048576 | tf_op jit(solution)/shard_map/all_to_all | solution.py:67
  150.2 1.3 convolution_convert_fusion.2
  151.5 1.3 convolution_convert_fusion.1
  152.7 1.3 convolution_convert_fusion
  154.0 26.3 %all-to-all-done.5 = f32[16,16,512]{2,1,0:T(8,128)} async-done(((f32[16,16,512]{2,1,0:T(8,128)}), f32[16,16,512]{2,1,0:T(8,128)}, u32[]{:S(2)}, u32[]{:S(2)}) %all-to-all-start.5) | async-done | bytes 524320 | tf_op jit(solution)/shard_map/all_to_all | solution.py:67
  180.3 1.7 reduce_sum.29
  (2 shorter events, 0.1 us)
Async XLA Ops:
  0.6 54.0 %copy-start = (bf16[512,512]{1,0:T(8,128)(2,1)S(1)}, bf16[512,512]{1,0:T(8,128)(2,1)}, u32[]{:S(2)}) copy-start(bf16[512,512]{1,0:T(8,128)(2,1)} %param.7) | copy-start | bytes 1572868
  48.8 4.8 %copy-start.1 = (bf16[512,512]{1,0:T(8,128)(2,1)S(1)}, bf16[512,512]{1,0:T(8,128)(2,1)}, u32[]{:S(2)}) copy-start(bf16[512,512]{1,0:T(8,128)(2,1)} %param.8) | copy-start | bytes 1572868
  48.9 5.2 %copy-start.3 = (bf16[512,512]{1,0:T(8,128)(2,1)S(1)}, bf16[512,512]{1,0:T(8,128)(2,1)}, u32[]{:S(2)}) copy-start(bf16[512,512]{1,0:T(8,128)(2,1)} %param.9) | copy-start | bytes 1572868
  135.2 1.0 copy-start.2
  144.4 35.9 %all-to-all-start.5 = ((f32[16,16,512]{2,1,0:T(8,128)}), f32[16,16,512]{2,1,0:T(8,128)}, u32[]{:S(2)}, u32[]{:S(2)}) async-start(f32[16,16,512]{2,1,0:T(8,128)} %reduce_sum.28), calls=%async_computation.5 | async-start | bytes 1048576 | tf_op jit(solution)/shard_map/all_to_all | solution.py:67

commit v6 on v4

--- a/solution.py
+++ b/solution.py
@@ -1,6 +1,7 @@
 import jax
 import jax.numpy as jnp
 from jax import lax
+from jax.experimental.layout import Layout, with_layout_constraint
 from jax.sharding import Mesh, PartitionSpec as P
 
 ROW = ("z", "core")
@@ -41,9 +42,10 @@
     )
     hid = gate_part.shape[1]
     chunk = n_tok // n_col
-    parts = jnp.stack([gate_part, up_part, grad_part]).reshape(3, n_col, chunk, hid)
-    parts = lax.all_to_all(parts, "col", 1, 1, tiled=True)
-    gate, up, hidden_grad = parts.sum(axis=1)
+    parts = jnp.stack([p.reshape(n_col, chunk, hid) for p in (gate_part, up_part, grad_part)], axis=1)
+    parts = with_layout_constraint(parts, Layout(major_to_minor=(0, 1, 2, 3)))
+    parts = lax.all_to_all(parts, "col", 0, 0, tiled=True)
+    gate, up, hidden_grad = parts.sum(axis=0)
     small = jnp.stack(pointwise(gate, up, hidden_grad))
     spread = jnp.broadcast_to(small[None], (n_col,) + small.shape)
     spread = lax.all_to_all(spread, "col", 0, 0, tiled=True)

time: 175 us -> 174 us (level)
  no operation moved by 1% of the time
where the time goes in v6:
time: 174 us
  blocking collectives  129 us (74%)
  waiting for transfers between devices  25.2 us (14%)
  matrix products  7.07 us (4%)
  starting transfers between devices  5.33 us (3%)
  other arithmetic  5.12 us (3%)
    all_to_all x1, blocking collectives, gather_rows(): mine = lax.all_to_all(both, ROW, 0, 0, tiled=True)  47.3 us
    all_to_all x1, blocking collectives, body(): parts = lax.all_to_all(parts, 'col', 0, 0, tiled=True)  46.9 us
    all_to_all x1, blocking collectives, body(): spread = lax.all_to_all(spread, 'col', 0, 0, tiled=True)  25.2 us
    all_to_all x1, waiting for transfers between devices, body(): input_grad = lax.all_to_all(total, 'z', 0, 0, tiled=True).sum(axis=0)  25.2 us
    all_to_all x1, starting transfers between devices, body(): input_grad = lax.all_to_all(total, 'z', 0, 0, tiled=True).sum(axis=0)  5.33 us
    all_to_all x1, blocking collectives, gather_rows(): full = lax.all_to_all(mine, 'core', 0, 0, tiled=True)  4.71 us
    all_to_all x1, blocking collectives, body(): total = lax.all_to_all(total, 'core', 0, 0, tiled=True).sum(axis=0)  4.58 us
  transfers between devices with their start and end apart: 1, of which 1 were waited for; matrix products, arithmetic and copies ran while one was open for 3% of the time, Pallas kernels for 0%

profile of v6, /device:TPU:32, one launch (start us, length us, event | category | flops | bytes accessed | tf_op | source)
XLA Modules:
  0.0 173.6 jit_solution(11144696341507704703)
XLA Ops:
  0.6 0.0 copy-start
  0.6 0.8 pad_maximum_fusion.2
  1.4 0.1 broadcast_in_dim.8
  1.5 47.3 %all_to_all.30 = bf16[32,16,512]{2,1,0:T(8,128)(2,1)S(1)} all-to-all(bf16[32,16,512]{2,1,0:T(8,128)(2,1)S(1)} %bitcast.53), channel_id=1, replica_groups=mesh['z'=16,'core'=2,'col'=16] {'z','core'}, dimensions={0} | all-to-all | bytes 1048576 | tf_op jit(solution)/shard_map/all_to_all | solution.py:23
  48.8 0.0 copy-start.1
  48.8 0.1 broadcast_in_dim.10
  48.9 4.7 %all_to_all.31 = bf16[2,512,512]{2,1,0:T(8,128)(2,1)S(1)} all-to-all(bf16[2,512,512]{2,1,0:T(8,128)(2,1)S(1)} %broadcast_in_dim.10), channel_id=1, replica_groups=mesh['z'=16,'core'=2,'col'=16] {'core'}, dimensions={0} | all-to-all | bytes 2097152 | tf_op jit(solution)/shard_map/all_to_all | solution.py:26
  53.6 0.0 copy-start.3
  53.6 0.1 fusion.11
  53.7 0.0 copy-done.1
  53.7 0.4 convolution_bitcast_fusion.1
  54.1 0.0 copy-done
  54.2 0.4 convolution_bitcast_fusion.2
  54.6 0.1 copy-done.3
  54.7 0.5 convolution_bitcast_fusion
  55.1 0.5 pad_maximum_fusion
  55.7 46.9 %all_to_all.32 = f32[16,3,32,512]{3,2,1,0:T(8,128)} all-to-all(f32[16,3,32,512]{3,2,1,0:T(8,128)S(1)} %pad_maximum_fusion), channel_id=1, replica_groups=mesh['z'=16,'core'=2,'col'=16] {'col'}, dimensions={0} | all-to-all | bytes 6291456 | tf_op jit(solution)/shard_map/all_to_all | solution.py:47
  102.5 2.2 %reduce_sum.27 = f32[3,32,512]{2,1,0:T(8,128)S(1)} reduce(f32[16,3,32,512]{3,2,1,0:T(8,128)} %all_to_all.32, f32[]{:T(128)} %constant.0.clone.1), dimensions={0}, to_apply=%region_0.0 | reduce | flops 737280 | bytes 3342340 | tf_op jit(solution)/shard_map/reduce_sum | solution.py:48
  104.8 0.2 broadcast_in_dim.22
  105.0 25.2 %all_to_all.33 = bf16[16,3,32,512]{3,2,1,0:T(8,128)(2,1)S(1)} all-to-all(bf16[16,3,32,512]{3,2,1,0:T(8,128)(2,1)S(1)} %broadcast_in_dim.22), channel_id=1, replica_groups=mesh['z'=16,'core'=2,'col'=16] {'col'}, dimensions={0} | all-to-all | bytes 3145728 | tf_op jit(solution)/shard_map/all_to_all | solution.py:51
  130.2 0.9 fusion.10
  131.1 0.0 copy-start.2
  131.1 0.5 fusion.12
  131.6 0.5 convolution_add_fusion
  132.1 0.1 copy.12
  132.2 0.0 copy-done.2
  132.2 4.6 %all_to_all.34 = f32[2,16,16,512]{3,2,1,0:T(8,128)S(1)} all-to-all(f32[2,16,16,512]{3,2,1,0:T(8,128)S(1)} %bitcast.51), channel_id=1, replica_groups=mesh['z'=16,'core'=2,'col'=16] {'core'}, dimensions={0} | all-to-all | bytes 2097152 | tf_op jit(solution)/shard_map/all_to_all | solution.py:68
  136.8 0.9 reduce_sum.28
  137.6 0.0 copy-start.4
  137.6 5.3 %all-to-all-start.5 = ((f32[16,16,512]{2,1,0:T(8,128)}), f32[16,16,512]{2,1,0:T(8,128)S(1)}, u32[]{:S(2)}, u32[]{:S(2)}) async-start(f32[16,16,512]{2,1,0:T(8,128)} %reduce_sum.28), calls=%async_computation.5 | async-start | bytes 1048576 | tf_op jit(solution)/shard_map/all_to_all | solution.py:69
  143.0 2.3 %convolution_convert_fusion.1 = bf16[512,512]{1,0:T(8,128)(2,1)} fusion(bf16[512,512]{1,0:T(8,128)(2,1)} %bitcast.57, bf16[2,512,512]{2,1,0:T(8,128)(2,1)S(1)} %all_to_all.31), kind=kOutput, calls=%fused_computation.6 | convolution fusion | flops 268697600 | bytes 1572864 | tf_op jit(solution)/shard_map/dot_general | solution.py:57
  145.3 1.3 convolution_convert_fusion.2
  146.5 0.0 copy-done.4
  146.5 1.3 convolution_convert_fusion
  147.8 25.2 %all-to-all-done.5 = f32[16,16,512]{2,1,0:T(8,128)S(1)} async-done(((f32[16,16,512]{2,1,0:T(8,128)}), f32[16,16,512]{2,1,0:T(8,128)S(1)}, u32[]{:S(2)}, u32[]{:S(2)}) %all-to-all-start.5) | async-done | bytes 524320 | tf_op jit(solution)/shard_map/all_to_all | solution.py:69
  173.0 0.6 reduce_sum.29
  (2 shorter events, 0.1 us)
Async XLA Ops:
  0.6 53.5 %copy-start = (bf16[512,512]{1,0:T(8,128)(2,1)S(1)}, bf16[512,512]{1,0:T(8,128)(2,1)}, u32[]{:S(2)}) copy-start(bf16[512,512]{1,0:T(8,128)(2,1)} %param.7) | copy-start | bytes 1572868
  48.8 4.9 %copy-start.1 = (bf16[512,512]{1,0:T(8,128)(2,1)S(1)}, bf16[512,512]{1,0:T(8,128)(2,1)}, u32[]{:S(2)}) copy-start(bf16[512,512]{1,0:T(8,128)(2,1)} %param.8) | copy-start | bytes 1572868
  53.6 1.0 copy-start.3
  131.1 1.1 copy-start.2
  137.6 8.9 %copy-start.4 = (bf16[1,16,32,512]{3,2,0,1:T(8,128)(2,1)S(1)}, bf16[1,16,32,512]{3,2,0,1:T(8,128)(2,1)}, u32[]{:S(2)}) copy-start(bf16[1,16,32,512]{3,2,0,1:T(8,128)(2,1)} %get-tuple-element.4) | copy-start | bytes 1572868
  137.6 35.3 %all-to-all-start.5 = ((f32[16,16,512]{2,1,0:T(8,128)}), f32[16,16,512]{2,1,0:T(8,128)S(1)}, u32[]{:S(2)}, u32[]{:S(2)}) async-start(f32[16,16,512]{2,1,0:T(8,128)} %reduce_sum.28), calls=%async_computation.5 | async-start | bytes 1048576 | tf_op jit(solution)/shard_map/all_to_all | solution.py:69

commit v7 on v6

--- a/solution.py
+++ b/solution.py
@@ -45,7 +45,8 @@
     parts = jnp.stack([p.reshape(n_col, chunk, hid) for p in (gate_part, up_part, grad_part)], axis=1)
     parts = with_layout_constraint(parts, Layout(major_to_minor=(0, 1, 2, 3)))
     parts = lax.all_to_all(parts, "col", 0, 0, tiled=True)
-    gate, up, hidden_grad = parts.sum(axis=0)
+    groups = parts.reshape((4, n_col // 4) + parts.shape[1:]).sum(axis=1)
+    gate, up, hidden_grad = lax.optimization_barrier(groups).sum(axis=0)
     small = jnp.stack(pointwise(gate, up, hidden_grad))
     spread = jnp.broadcast_to(small[None], (n_col,) + small.shape)
     spread = lax.all_to_all(spread, "col", 0, 0, tiled=True)

time: 174 us -> 172 us (0.989)
  other arithmetic: 5.12 us -> 3.36 us
    reduce_sum x1 -> x2, other arithmetic: 2.19 us -> 0.43 us  [the longest x1 0.37 us: body(): groups = parts.reshape((4, n_col // 4) + parts.shape[1:]).sum(axis=1)]
where the time goes in v7:
time: 172 us
  blocking collectives  129 us (75%)
  waiting for transfers between devices  25.2 us (15%)
  matrix products  7.07 us (4%)
  starting transfers between devices  5.34 us (3%)
  other arithmetic  3.36 us (2%)
    all_to_all x1, blocking collectives, gather_rows(): mine = lax.all_to_all(both, ROW, 0, 0, tiled=True)  47.3 us
    all_to_all x1, blocking collectives, body(): parts = lax.all_to_all(parts, 'col', 0, 0, tiled=True)  46.8 us
    all_to_all x1, blocking collectives, body(): spread = lax.all_to_all(spread, 'col', 0, 0, tiled=True)  25.2 us
    all_to_all x1, waiting for transfers between devices, body(): input_grad = lax.all_to_all(total, 'z', 0, 0, tiled=True).sum(axis=0)  25.2 us
    all_to_all x1, starting transfers between devices, body(): input_grad = lax.all_to_all(total, 'z', 0, 0, tiled=True).sum(axis=0)  5.34 us
    all_to_all x1, blocking collectives, gather_rows(): full = lax.all_to_all(mine, 'core', 0, 0, tiled=True)  4.71 us
    all_to_all x1, blocking collectives, body(): total = lax.all_to_all(total, 'core', 0, 0, tiled=True).sum(axis=0)  4.58 us
  transfers between devices with their start and end apart: 1, of which 1 were waited for; matrix products, arithmetic and copies ran while one was open for 3% of the time, Pallas kernels for 0%

profile of v7, /device:TPU:32, one launch (start us, length us, event | category | flops | bytes accessed | tf_op | source)
XLA Modules:
  0.0 171.8 jit_solution(1803558264885795204)
XLA Ops:
  0.6 0.0 copy-start
  0.6 0.8 pad_maximum_fusion.2
  1.4 0.1 broadcast_in_dim.8
  1.5 47.3 %all_to_all.30 = bf16[32,16,512]{2,1,0:T(8,128)(2,1)S(1)} all-to-all(bf16[32,16,512]{2,1,0:T(8,128)(2,1)S(1)} %bitcast.55), channel_id=1, replica_groups=mesh['z'=16,'core'=2,'col'=16] {'z','core'}, dimensions={0} | all-to-all | bytes 1048576 | tf_op jit(solution)/shard_map/all_to_all | solution.py:23
  48.8 0.0 copy-start.1
  48.8 0.1 broadcast_in_dim.10
  48.9 4.7 %all_to_all.31 = bf16[2,512,512]{2,1,0:T(8,128)(2,1)S(1)} all-to-all(bf16[2,512,512]{2,1,0:T(8,128)(2,1)S(1)} %broadcast_in_dim.10), channel_id=1, replica_groups=mesh['z'=16,'core'=2,'col'=16] {'core'}, dimensions={0} | all-to-all | bytes 2097152 | tf_op jit(solution)/shard_map/all_to_all | solution.py:26
  53.6 0.0 copy-start.3
  53.6 0.1 fusion.11
  53.7 0.0 copy-done.1
  53.7 0.4 convolution_bitcast_fusion.1
  54.1 0.0 copy-done
  54.2 0.4 convolution_bitcast_fusion.2
  54.6 0.1 copy-done.3
  54.7 0.5 convolution_bitcast_fusion
  55.1 0.5 pad_maximum_fusion
  55.7 46.8 %all_to_all.32 = f32[16,3,32,512]{3,2,1,0:T(8,128)S(1)} all-to-all(f32[16,3,32,512]{3,2,1,0:T(8,128)S(1)} %pad_maximum_fusion), channel_id=1, replica_groups=mesh['z'=16,'core'=2,'col'=16] {'col'}, dimensions={0} | all-to-all | bytes 6291456 | tf_op jit(solution)/shard_map/all_to_all | solution.py:47
  102.4 0.4 bitcast_reduce_fusion
  102.8 0.1 reduce_sum.37
  103.0 0.2 broadcast_in_dim.22
  103.1 25.2 %all_to_all.33 = bf16[16,3,32,512]{3,2,1,0:T(8,128)(2,1)S(1)} all-to-all(bf16[16,3,32,512]{3,2,1,0:T(8,128)(2,1)S(1)} %broadcast_in_dim.22), channel_id=1, replica_groups=mesh['z'=16,'core'=2,'col'=16] {'col'}, dimensions={0} | all-to-all | bytes 3145728 | tf_op jit(solution)/shard_map/all_to_all | solution.py:52
  128.4 0.9 fusion.10
  129.3 0.0 copy-start.2
  129.3 0.5 fusion.12
  129.7 0.5 convolution_add_fusion
  130.2 0.1 copy.12
  130.3 0.0 copy-done.2
  130.3 4.6 %all_to_all.34 = f32[2,16,16,512]{3,2,1,0:T(8,128)S(1)} all-to-all(f32[2,16,16,512]{3,2,1,0:T(8,128)S(1)} %bitcast.53), channel_id=1, replica_groups=mesh['z'=16,'core'=2,'col'=16] {'core'}, dimensions={0} | all-to-all | bytes 2097152 | tf_op jit(solution)/shard_map/all_to_all | solution.py:69
  134.9 0.9 reduce_sum.38
  135.8 0.0 copy-start.4
  135.8 5.3 %all-to-all-start.5 = ((f32[16,16,512]{2,1,0:T(8,128)}), f32[16,16,512]{2,1,0:T(8,128)S(1)}, u32[]{:S(2)}, u32[]{:S(2)}) async-start(f32[16,16,512]{2,1,0:T(8,128)} %reduce_sum.38), calls=%async_computation.5 | async-start | bytes 1048576 | tf_op jit(solution)/shard_map/all_to_all | solution.py:70
  141.1 2.3 %convolution_convert_fusion.1 = bf16[512,512]{1,0:T(8,128)(2,1)} fusion(bf16[512,512]{1,0:T(8,128)(2,1)} %bitcast.59, bf16[2,512,512]{2,1,0:T(8,128)(2,1)S(1)} %all_to_all.31), kind=kOutput, calls=%fused_computation.7 | convolution fusion | flops 268697600 | bytes 1572864 | tf_op jit(solution)/shard_map/dot_general | solution.py:58
  143.4 1.3 convolution_convert_fusion.2
  144.7 0.0 copy-done.4
  144.7 1.3 convolution_convert_fusion
  145.9 25.2 %all-to-all-done.5 = f32[16,16,512]{2,1,0:T(8,128)S(1)} async-done(((f32[16,16,512]{2,1,0:T(8,128)}), f32[16,16,512]{2,1,0:T(8,128)S(1)}, u32[]{:S(2)}, u32[]{:S(2)}) %all-to-all-start.5) | async-done | bytes 524320 | tf_op jit(solution)/shard_map/all_to_all | solution.py:70
  171.1 0.6 reduce_sum.39
  (2 shorter events, 0.1 us)
Async XLA Ops:
  0.6 53.5 %copy-start = (bf16[512,512]{1,0:T(8,128)(2,1)S(1)}, bf16[512,512]{1,0:T(8,128)(2,1)}, u32[]{:S(2)}) copy-start(bf16[512,512]{1,0:T(8,128)(2,1)} %param.7) | copy-start | bytes 1572868
  48.8 4.9 %copy-start.1 = (bf16[512,512]{1,0:T(8,128)(2,1)S(1)}, bf16[512,512]{1,0:T(8,128)(2,1)}, u32[]{:S(2)}) copy-start(bf16[512,512]{1,0:T(8,128)(2,1)} %param.8) | copy-start | bytes 1572868
  53.6 1.0 copy-start.3
  129.3 1.1 copy-start.2
  135.8 8.9 %copy-start.4 = (bf16[1,16,32,512]{3,2,0,1:T(8,128)(2,1)S(1)}, bf16[1,16,32,512]{3,2,0,1:T(8,128)(2,1)}, u32[]{:S(2)}) copy-start(bf16[1,16,32,512]{3,2,0,1:T(8,128)(2,1)} %get-tuple-element.4) | copy-start | bytes 1572868
  135.8 35.3 %all-to-all-start.5 = ((f32[16,16,512]{2,1,0:T(8,128)}), f32[16,16,512]{2,1,0:T(8,128)S(1)}, u32[]{:S(2)}, u32[]{:S(2)}) async-start(f32[16,16,512]{2,1,0:T(8,128)} %reduce_sum.38), calls=%async_computation.5 | async-start | bytes 1048576 | tf_op jit(solution)/shard_map/all_to_all | solution.py:70

commit v8 on v7

--- a/solution.py
+++ b/solution.py
@@ -67,7 +67,9 @@
     block = n_tok // (n_z * n_core)
     total = total.reshape(n_z, n_core, block, width).transpose(1, 0, 2, 3)
     total = lax.all_to_all(total, "core", 0, 0, tiled=True).sum(axis=0)
-    input_grad = lax.all_to_all(total, "z", 0, 0, tiled=True).sum(axis=0)
+    total = lax.all_to_all(total, "z", 0, 0, tiled=True)
+    total = total.reshape((4, n_z // 4) + total.shape[1:]).sum(axis=1)
+    input_grad = lax.optimization_barrier(total).sum(axis=0)
     return (input_grad.astype(jnp.bfloat16), gate_weight_grad, up_weight_grad, down_weight_grad)
 
 

time: 172 us -> 172 us (level)
  no operation moved by 1% of the time
where the time goes in v8:
time: 172 us
  blocking collectives  129 us (75%)
  waiting for transfers between devices  25.2 us (15%)
  matrix products  7.07 us (4%)
  starting transfers between devices  5.34 us (3%)
  other arithmetic  3.38 us (2%)
    all_to_all x1, blocking collectives, gather_rows(): mine = lax.all_to_all(both, ROW, 0, 0, tiled=True)  47.3 us
    all_to_all x1, blocking collectives, body(): parts = lax.all_to_all(parts, 'col', 0, 0, tiled=True)  46.8 us
    all_to_all x1, blocking collectives, body(): spread = lax.all_to_all(spread, 'col', 0, 0, tiled=True)  25.2 us
    all_to_all x1, waiting for transfers between devices, body(): total = lax.all_to_all(total, 'z', 0, 0, tiled=True)  25.2 us
    all_to_all x1, starting transfers between devices, body(): total = lax.all_to_all(total, 'z', 0, 0, tiled=True)  5.34 us
    all_to_all x1, blocking collectives, gather_rows(): full = lax.all_to_all(mine, 'core', 0, 0, tiled=True)  4.71 us
    all_to_all x1, blocking collectives, body(): total = lax.all_to_all(total, 'core', 0, 0, tiled=True).sum(axis=0)  4.58 us
  transfers between devices with their start and end apart: 1, of which 1 were waited for; matrix products, arithmetic and copies ran while one was open for 3% of the time, Pallas kernels for 0%

profile of v8, /device:TPU:32, one launch (start us, length us, event | category | flops | bytes accessed | tf_op | source)
XLA Modules:
  0.0 171.8 jit_solution(4194519832112357594)
XLA Ops:
  0.6 0.0 copy-start
  0.6 0.8 pad_maximum_fusion.2
  1.4 0.1 broadcast_in_dim.8
  1.5 47.3 %all_to_all.30 = bf16[32,16,512]{2,1,0:T(8,128)(2,1)S(1)} all-to-all(bf16[32,16,512]{2,1,0:T(8,128)(2,1)S(1)} %bitcast.57), channel_id=1, replica_groups=mesh['z'=16,'core'=2,'col'=16] {'z','core'}, dimensions={0} | all-to-all | bytes 1048576 | tf_op jit(solution)/shard_map/all_to_all | solution.py:23
  48.8 0.0 copy-start.1
  48.8 0.1 broadcast_in_dim.10
  48.9 4.7 %all_to_all.31 = bf16[2,512,512]{2,1,0:T(8,128)(2,1)S(1)} all-to-all(bf16[2,512,512]{2,1,0:T(8,128)(2,1)S(1)} %broadcast_in_dim.10), channel_id=1, replica_groups=mesh['z'=16,'core'=2,'col'=16] {'core'}, dimensions={0} | all-to-all | bytes 2097152 | tf_op jit(solution)/shard_map/all_to_all | solution.py:26
  53.6 0.0 copy-start.3
  53.6 0.1 fusion.11
  53.7 0.0 copy-done.1
  53.7 0.4 convolution_bitcast_fusion.1
  54.1 0.0 copy-done
  54.2 0.4 convolution_bitcast_fusion.2
  54.6 0.1 copy-done.3
  54.7 0.5 convolution_bitcast_fusion
  55.1 0.5 pad_maximum_fusion
  55.7 46.8 %all_to_all.32 = f32[16,3,32,512]{3,2,1,0:T(8,128)S(1)} all-to-all(f32[16,3,32,512]{3,2,1,0:T(8,128)S(1)} %pad_maximum_fusion), channel_id=1, replica_groups=mesh['z'=16,'core'=2,'col'=16] {'col'}, dimensions={0} | all-to-all | bytes 6291456 | tf_op jit(solution)/shard_map/all_to_all | solution.py:47
  102.4 0.4 bitcast_reduce_fusion
  102.8 0.1 reduce_sum.46
  103.0 0.2 broadcast_in_dim.22
  103.1 25.2 %all_to_all.33 = bf16[16,3,32,512]{3,2,1,0:T(8,128)(2,1)S(1)} all-to-all(bf16[16,3,32,512]{3,2,1,0:T(8,128)(2,1)S(1)} %broadcast_in_dim.22), channel_id=1, replica_groups=mesh['z'=16,'core'=2,'col'=16] {'col'}, dimensions={0} | all-to-all | bytes 3145728 | tf_op jit(solution)/shard_map/all_to_all | solution.py:52
  128.4 0.9 fusion.10
  129.3 0.0 copy-start.2
  129.3 0.5 fusion.12
  129.7 0.5 convolution_add_fusion
  130.2 0.1 copy.12
  130.3 0.0 copy-done.2
  130.3 4.6 %all_to_all.34 = f32[2,16,16,512]{3,2,1,0:T(8,128)S(1)} all-to-all(f32[2,16,16,512]{3,2,1,0:T(8,128)S(1)} %bitcast.55), channel_id=1, replica_groups=mesh['z'=16,'core'=2,'col'=16] {'core'}, dimensions={0} | all-to-all | bytes 2097152 | tf_op jit(solution)/shard_map/all_to_all | solution.py:69
  134.9 0.9 reduce_sum.47
  135.8 0.0 copy-start.4
  135.8 5.3 %all-to-all-start.5 = ((f32[16,16,512]{2,1,0:T(8,128)}), f32[16,16,512]{2,1,0:T(8,128)S(1)}, u32[]{:S(2)}, u32[]{:S(2)}) async-start(f32[16,16,512]{2,1,0:T(8,128)} %reduce_sum.47), calls=%async_computation.5 | async-start | bytes 1048576 | tf_op jit(solution)/shard_map/all_to_all | solution.py:70
  141.1 2.3 %convolution_convert_fusion.1 = bf16[512,512]{1,0:T(8,128)(2,1)} fusion(bf16[512,512]{1,0:T(8,128)(2,1)} %bitcast.61, bf16[2,512,512]{2,1,0:T(8,128)(2,1)S(1)} %all_to_all.31), kind=kOutput, calls=%fused_computation.7 | convolution fusion | flops 268697600 | bytes 1572864 | tf_op jit(solution)/shard_map/dot_general | solution.py:58
  143.4 1.3 convolution_convert_fusion.2
  144.7 0.0 copy-done.4
  144.7 1.3 convolution_convert_fusion
  145.9 25.2 %all-to-all-done.5 = f32[16,16,512]{2,1,0:T(8,128)S(1)} async-done(((f32[16,16,512]{2,1,0:T(8,128)}), f32[16,16,512]{2,1,0:T(8,128)S(1)}, u32[]{:S(2)}, u32[]{:S(2)}) %all-to-all-start.5) | async-done | bytes 524320 | tf_op jit(solution)/shard_map/all_to_all | solution.py:70
  171.2 0.6 reduce_sum.49
  (3 shorter events, 0.1 us)
Async XLA Ops:
  0.6 53.5 %copy-start = (bf16[512,512]{1,0:T(8,128)(2,1)S(1)}, bf16[512,512]{1,0:T(8,128)(2,1)}, u32[]{:S(2)}) copy-start(bf16[512,512]{1,0:T(8,128)(2,1)} %param.7) | copy-start | bytes 1572868
  48.8 4.9 %copy-start.1 = (bf16[512,512]{1,0:T(8,128)(2,1)S(1)}, bf16[512,512]{1,0:T(8,128)(2,1)}, u32[]{:S(2)}) copy-start(bf16[512,512]{1,0:T(8,128)(2,1)} %param.8) | copy-start | bytes 1572868
  53.6 1.0 copy-start.3
  129.3 1.1 copy-start.2
  135.8 8.9 %copy-start.4 = (bf16[1,16,32,512]{3,2,0,1:T(8,128)(2,1)S(1)}, bf16[1,16,32,512]{3,2,0,1:T(8,128)(2,1)}, u32[]{:S(2)}) copy-start(bf16[1,16,32,512]{3,2,0,1:T(8,128)(2,1)} %get-tuple-element.4) | copy-start | bytes 1572868
  135.8 35.3 %all-to-all-start.5 = ((f32[16,16,512]{2,1,0:T(8,128)}), f32[16,16,512]{2,1,0:T(8,128)S(1)}, u32[]{:S(2)}, u32[]{:S(2)}) async-start(f32[16,16,512]{2,1,0:T(8,128)} %reduce_sum.47), calls=%async_computation.5 | async-start | bytes 1048576 | tf_op jit(solution)/shard_map/all_to_all | solution.py:70

commit v9 on v7

--- a/solution.py
+++ b/solution.py
@@ -66,7 +66,8 @@
     ) + lax.dot_general(up_grad, up_weight, contract_cols, preferred_element_type=jnp.float32)
     block = n_tok // (n_z * n_core)
     total = total.reshape(n_z, n_core, block, width).transpose(1, 0, 2, 3)
-    total = lax.all_to_all(total, "core", 0, 0, tiled=True).sum(axis=0)
+    total = lax.all_to_all(total, "core", 0, 0, tiled=True)
+    total = total[0] + total[1]
     input_grad = lax.all_to_all(total, "z", 0, 0, tiled=True).sum(axis=0)
     return (input_grad.astype(jnp.bfloat16), gate_weight_grad, up_weight_grad, down_weight_grad)
 

time: 172 us -> 172 us (level)
  transfers between devices with their start and end apart: 1 -> 1, of which waited for: 1 -> 1; matrix products, arithmetic and copies ran while one was open for 3% -> 2% of each run, Pallas kernels for 0% -> 0%
where the time goes in v9:
time: 172 us
  blocking collectives  129 us (75%)
  waiting for transfers between devices  26.2 us (15%)
  matrix products  6.03 us (4%)
  starting transfers between devices  5.2 us (3%)
  other arithmetic  3.35 us (2%)
    all_to_all x1, blocking collectives, gather_rows(): mine = lax.all_to_all(both, ROW, 0, 0, tiled=True)  47.3 us
    all_to_all x1, blocking collectives, body(): parts = lax.all_to_all(parts, 'col', 0, 0, tiled=True)  46.8 us
    all_to_all x1, waiting for transfers between devices, body(): input_grad = lax.all_to_all(total, 'z', 0, 0, tiled=True).sum(axis=0)  26.2 us
    all_to_all x1, blocking collectives, body(): spread = lax.all_to_all(spread, 'col', 0, 0, tiled=True)  25.2 us
    all_to_all x1, starting transfers between devices, body(): input_grad = lax.all_to_all(total, 'z', 0, 0, tiled=True).sum(axis=0)  5.2 us
    all_to_all x1, blocking collectives, gather_rows(): full = lax.all_to_all(mine, 'core', 0, 0, tiled=True)  4.71 us
    all_to_all x1, blocking collectives, body(): total = lax.all_to_all(total, 'core', 0, 0, tiled=True)  4.71 us
  transfers between devices with their start and end apart: 1, of which 1 were waited for; matrix products, arithmetic and copies ran while one was open for 2% of the time, Pallas kernels for 0%

profile of v9, /device:TPU:32, one launch (start us, length us, event | category | flops | bytes accessed | tf_op | source)
XLA Modules:
  0.0 171.8 jit_solution(16696292931999616888)
XLA Ops:
  0.6 0.0 copy-start
  0.6 0.8 pad_maximum_fusion.2
  1.4 0.1 broadcast_in_dim.8
  1.5 47.3 %all_to_all.30 = bf16[32,16,512]{2,1,0:T(8,128)(2,1)S(1)} all-to-all(bf16[32,16,512]{2,1,0:T(8,128)(2,1)S(1)} %bitcast.57), channel_id=1, replica_groups=mesh['z'=16,'core'=2,'col'=16] {'z','core'}, dimensions={0} | all-to-all | bytes 1048576 | tf_op jit(solution)/shard_map/all_to_all | solution.py:23
  48.8 0.0 copy-start.1
  48.8 0.1 broadcast_in_dim.10
  48.9 4.7 %all_to_all.31 = bf16[2,512,512]{2,1,0:T(8,128)(2,1)S(1)} all-to-all(bf16[2,512,512]{2,1,0:T(8,128)(2,1)S(1)} %broadcast_in_dim.10), channel_id=1, replica_groups=mesh['z'=16,'core'=2,'col'=16] {'core'}, dimensions={0} | all-to-all | bytes 2097152 | tf_op jit(solution)/shard_map/all_to_all | solution.py:26
  53.6 0.0 copy-start.4
  53.6 0.1 fusion.12
  53.7 0.0 copy-done.1
  53.7 0.4 convolution_bitcast_fusion.1
  54.1 0.0 copy-done
  54.2 0.4 convolution_bitcast_fusion.2
  54.6 0.1 copy-done.4
  54.7 0.5 convolution_bitcast_fusion
  55.1 0.5 pad_maximum_fusion
  55.7 46.8 %all_to_all.32 = f32[16,3,32,512]{3,2,1,0:T(8,128)S(1)} all-to-all(f32[16,3,32,512]{3,2,1,0:T(8,128)S(1)} %pad_maximum_fusion), channel_id=1, replica_groups=mesh['z'=16,'core'=2,'col'=16] {'col'}, dimensions={0} | all-to-all | bytes 6291456 | tf_op jit(solution)/shard_map/all_to_all | solution.py:47
  102.4 0.4 bitcast_reduce_fusion
  102.8 0.1 reduce_sum.28
  103.0 0.2 broadcast_in_dim.22
  103.1 25.2 %all_to_all.33 = bf16[16,3,32,512]{3,2,1,0:T(8,128)(2,1)S(1)} all-to-all(bf16[16,3,32,512]{3,2,1,0:T(8,128)(2,1)S(1)} %broadcast_in_dim.22), channel_id=1, replica_groups=mesh['z'=16,'core'=2,'col'=16] {'col'}, dimensions={0} | all-to-all | bytes 3145728 | tf_op jit(solution)/shard_map/all_to_all | solution.py:52
  128.4 0.9 fusion.11
  129.3 0.0 copy-start.2
  129.3 0.5 fusion.13
  129.7 0.5 convolution_add_fusion
  130.2 0.1 copy.11
  130.3 0.0 copy-done.2
  130.3 0.0 copy-start.3
  130.3 4.7 %all_to_all.34 = f32[2,16,16,512]{3,2,1,0:T(8,128)S(1)} all-to-all(f32[2,16,16,512]{3,2,1,0:T(8,128)S(1)} %bitcast.55), channel_id=1, replica_groups=mesh['z'=16,'core'=2,'col'=16] {'core'}, dimensions={0} | all-to-all | bytes 2097152 | tf_op jit(solution)/shard_map/all_to_all | solution.py:69
  135.0 0.9 fusion
  135.9 5.2 %all-to-all-start.5 = ((f32[16,16,512]{2,1,0:T(8,128)}), f32[16,16,512]{2,1,0:T(8,128)S(1)}, u32[]{:S(2)}, u32[]{:S(2)}) async-start(f32[16,16,512]{2,1,0:T(8,128)} %fusion), calls=%async_computation.5 | async-start | bytes 1048576 | tf_op jit(solution)/shard_map/all_to_all | solution.py:71
  141.1 0.0 copy-done.3
  141.1 0.0 copy-start.5
  141.1 1.3 convolution_convert_fusion.1
  142.4 1.3 convolution_convert_fusion.2
  143.7 0.0 copy-done.5
  143.7 1.3 convolution_convert_fusion
  144.9 26.2 %all-to-all-done.5 = f32[16,16,512]{2,1,0:T(8,128)S(1)} async-done(((f32[16,16,512]{2,1,0:T(8,128)}), f32[16,16,512]{2,1,0:T(8,128)S(1)}, u32[]{:S(2)}, u32[]{:S(2)}) %all-to-all-start.5) | async-done | bytes 524320 | tf_op jit(solution)/shard_map/all_to_all | solution.py:71
  171.1 0.6 reduce_sum.29
  (2 shorter events, 0.1 us)
Async XLA Ops:
  0.6 53.5 %copy-start = (bf16[512,512]{1,0:T(8,128)(2,1)S(1)}, bf16[512,512]{1,0:T(8,128)(2,1)}, u32[]{:S(2)}) copy-start(bf16[512,512]{1,0:T(8,128)(2,1)} %param.7) | copy-start | bytes 1572868
  48.8 4.9 %copy-start.1 = (bf16[512,512]{1,0:T(8,128)(2,1)S(1)}, bf16[512,512]{1,0:T(8,128)(2,1)}, u32[]{:S(2)}) copy-start(bf16[512,512]{1,0:T(8,128)(2,1)} %param.8) | copy-start | bytes 1572868
  53.6 1.0 copy-start.4
  129.3 1.1 copy-start.2
  130.3 10.8 %copy-start.3 = (bf16[1,16,32,512]{3,2,0,1:T(8,128)(2,1)S(1)}, bf16[1,16,32,512]{3,2,0,1:T(8,128)(2,1)}, u32[]{:S(2)}) copy-start(bf16[1,16,32,512]{3,2,0,1:T(8,128)(2,1)} %copy-done.2) | copy-start | bytes 1572868
  135.9 35.2 %all-to-all-start.5 = ((f32[16,16,512]{2,1,0:T(8,128)}), f32[16,16,512]{2,1,0:T(8,128)S(1)}, u32[]{:S(2)}, u32[]{:S(2)}) async-start(f32[16,16,512]{2,1,0:T(8,128)} %fusion), calls=%async_computation.5 | async-start | bytes 1048576 | tf_op jit(solution)/shard_map/all_to_all | solution.py:71
  141.1 2.5 %copy-start.5 = (bf16[1,16,32,512]{3,2,0,1:T(8,128)(2,1)S(1)}, bf16[1,16,32,512]{3,2,0,1:T(8,128)(2,1)}, u32[]{:S(2)}) copy-start(bf16[1,16,32,512]{3,2,0,1:T(8,128)(2,1)} %get-tuple-element.4) | copy-start | bytes 1572868

commit v10 on v9

--- a/solution.py
+++ b/solution.py
@@ -47,11 +47,10 @@
     parts = lax.all_to_all(parts, "col", 0, 0, tiled=True)
     groups = parts.reshape((4, n_col // 4) + parts.shape[1:]).sum(axis=1)
     gate, up, hidden_grad = lax.optimization_barrier(groups).sum(axis=0)
-    small = jnp.stack(pointwise(gate, up, hidden_grad))
+    small = jnp.concatenate(pointwise(gate, up, hidden_grad), axis=1)
     spread = jnp.broadcast_to(small[None], (n_col,) + small.shape)
-    spread = lax.all_to_all(spread, "col", 0, 0, tiled=True)
-    spread = spread.transpose(1, 0, 2, 3).reshape(3, n_tok, hid)
-    hidden, gate_grad, up_grad = spread[0], spread[1], spread[2]
+    spread = lax.all_to_all(spread, "col", 0, 0, tiled=True).reshape(n_tok, 3 * hid)
+    hidden, gate_grad, up_grad = spread[:, :hid], spread[:, hid:2 * hid], spread[:, 2 * hid:]
     gate_weight_grad = lax.dot_general(
         rows_all, gate_grad, contract_rows, preferred_element_type=jnp.float32
     ).astype(jnp.bfloat16)

time: 172 us -> 175 us (1.017)
    unnamed x12 -> x8, local copies, waits for them, and re-layouts: 0.1 us -> 2.15 us
where the time goes in v10:
time: 175 us; the launch traced here: 174 us
  blocking collectives  128 us (73%)
  waiting for transfers between devices  26.3 us (15%)
  matrix products  6.02 us (3%)
  starting transfers between devices  5.8 us (3%)
  other arithmetic  4.41 us (3%)
  local copies, waits for them, and re-layouts  2.58 us (1%)
    all_to_all x1, blocking collectives, gather_rows(): mine = lax.all_to_all(both, ROW, 0, 0, tiled=True)  47.3 us
    all_to_all x1, blocking collectives, body(): parts = lax.all_to_all(parts, 'col', 0, 0, tiled=True)  46.8 us
    all_to_all x1, waiting for transfers between devices, body(): input_grad = lax.all_to_all(total, 'z', 0, 0, tiled=True).sum(axis=0)  26.3 us
    all_to_all x1, blocking collectives, body(): lax.all_to_all(spread, 'col', 0, 0, tiled=True).reshape(n_tok, 3 * hid)  25.2 us
    all_to_all x1, starting transfers between devices, body(): input_grad = lax.all_to_all(total, 'z', 0, 0, tiled=True).sum(axis=0)  5.8 us
    all_to_all x1, blocking collectives, gather_rows(): full = lax.all_to_all(mine, 'core', 0, 0, tiled=True)  4.58 us
    all_to_all x1, blocking collectives, body(): total = lax.all_to_all(total, 'core', 0, 0, tiled=True)  4.58 us
  transfers between devices with their start and end apart: 1, of which 1 were waited for; matrix products, arithmetic and copies ran while one was open for 2% of the time, Pallas kernels for 0%

profile of v10, /device:TPU:32, one launch (start us, length us, event | category | flops | bytes accessed | tf_op | source)
XLA Modules:
  0.0 174.4 jit_solution(10318547561649466147)
XLA Ops:
  0.6 0.0 copy-start
  0.6 0.8 pad_maximum_fusion.2
  1.4 0.1 broadcast_in_dim.8
  1.5 47.3 %all_to_all.30 = bf16[32,16,512]{2,1,0:T(8,128)(2,1)S(1)} all-to-all(bf16[32,16,512]{2,1,0:T(8,128)(2,1)S(1)} %bitcast.75), channel_id=1, replica_groups=mesh['z'=16,'core'=2,'col'=16] {'z','core'}, dimensions={0} | all-to-all | bytes 1048576 | tf_op jit(solution)/shard_map/all_to_all | solution.py:23
  48.8 0.1 broadcast_in_dim.10
  48.9 4.6 %all_to_all.31 = bf16[2,512,512]{2,1,0:T(8,128)(2,1)S(1)} all-to-all(bf16[2,512,512]{2,1,0:T(8,128)(2,1)S(1)} %broadcast_in_dim.10), channel_id=1, replica_groups=mesh['z'=16,'core'=2,'col'=16] {'core'}, dimensions={0} | all-to-all | bytes 2097152 | tf_op jit(solution)/shard_map/all_to_all | solution.py:26
  53.5 0.0 copy-start.1
  53.5 0.1 fusion.17
  53.6 1.0 copy-done.1
  54.5 0.4 convolution_bitcast_fusion.1
  55.0 0.0 copy-done
  55.0 0.0 copy-start.3
  55.0 0.4 convolution_bitcast_fusion.2
  55.4 0.6 copy-done.3
  56.0 0.5 convolution_bitcast_fusion
  56.5 0.5 pad_maximum_fusion
  57.0 46.8 %all_to_all.32 = f32[16,3,32,512]{3,2,1,0:T(8,128)S(1)} all-to-all(f32[16,3,32,512]{3,2,1,0:T(8,128)S(1)} %pad_maximum_fusion), channel_id=1, replica_groups=mesh['z'=16,'core'=2,'col'=16] {'col'}, dimensions={0} | all-to-all | bytes 6291456 | tf_op jit(solution)/shard_map/all_to_all | solution.py:47
  103.8 0.4 bitcast_reduce_fusion
  104.2 0.1 reduce_sum.28
  104.2 0.1 multiply_convert_fusion.2
  104.3 0.1 broadcast_in_dim.22
  104.5 25.2 %all_to_all.33 = bf16[16,32,1536]{2,1,0:T(8,128)(2,1)S(1)} all-to-all(bf16[16,32,1536]{2,1,0:T(8,128)(2,1)S(1)} %broadcast_in_dim.22), channel_id=1, replica_groups=mesh['z'=16,'core'=2,'col'=16] {'col'}, dimensions={0} | all-to-all | bytes 3145728 | tf_op jit(solution)/shard_map/all_to_all | solution.py:52
  129.7 0.0 copy-start.2
  129.7 0.5 fusion.11
  130.2 0.6 copy-done.2
  130.7 0.5 convolution_add_fusion
  131.2 0.1 copy.11
  131.3 4.6 %all_to_all.34 = f32[2,16,16,512]{3,2,1,0:T(8,128)S(1)} all-to-all(f32[2,16,16,512]{3,2,1,0:T(8,128)S(1)} %bitcast.73), channel_id=1, replica_groups=mesh['z'=16,'core'=2,'col'=16] {'core'}, dimensions={0} | all-to-all | bytes 2097152 | tf_op jit(solution)/shard_map/all_to_all | solution.py:68
  135.9 0.9 fusion.1
  136.8 5.8 %all-to-all-start.5 = ((f32[16,16,512]{2,1,0:T(8,128)}), f32[16,16,512]{2,1,0:T(8,128)}, u32[]{:S(2)}, u32[]{:S(2)}) async-start(f32[16,16,512]{2,1,0:T(8,128)} %fusion.1), calls=%async_computation.5 | async-start | bytes 1048576 | tf_op jit(solution)/shard_map/all_to_all | solution.py:70
  142.6 1.3 convolution_convert_fusion.2
  143.8 1.3 convolution_convert_fusion.1
  145.1 1.3 convolution_convert_fusion
  146.3 26.3 %all-to-all-done.5 = f32[16,16,512]{2,1,0:T(8,128)} async-done(((f32[16,16,512]{2,1,0:T(8,128)}), f32[16,16,512]{2,1,0:T(8,128)}, u32[]{:S(2)}, u32[]{:S(2)}) %all-to-all-start.5) | async-done | bytes 524320 | tf_op jit(solution)/shard_map/all_to_all | solution.py:70
  172.7 1.7 reduce_sum.29
  (1 shorter events, 0.0 us)
Async XLA Ops:
  0.6 54.3 %copy-start = (bf16[512,512]{1,0:T(8,128)(2,1)S(1)}, bf16[512,512]{1,0:T(8,128)(2,1)}, u32[]{:S(2)}) copy-start(bf16[512,512]{1,0:T(8,128)(2,1)} %param.7) | copy-start | bytes 1572868
  53.5 1.0 copy-start.1
  55.0 1.0 copy-start.3
  129.7 1.0 copy-start.2
  136.8 35.9 %all-to-all-start.5 = ((f32[16,16,512]{2,1,0:T(8,128)}), f32[16,16,512]{2,1,0:T(8,128)}, u32[]{:S(2)}, u32[]{:S(2)}) async-start(f32[16,16,512]{2,1,0:T(8,128)} %fusion.1), calls=%async_computation.5 | async-start | bytes 1048576 | tf_op jit(solution)/shard_map/all_to_all | solution.py:70

commit v11 on v9

--- a/solution.py
+++ b/solution.py
@@ -17,8 +17,9 @@
 
 
 def gather_rows(tokens, out_grad, n_z, n_core):
-    both = jnp.stack([tokens, out_grad])
-    both = jnp.broadcast_to(both[None], (n_z,) + both.shape)
+    shape = (n_z, n_core) + tokens.shape
+    to_core = lax.broadcasted_iota(jnp.int32, shape, 1)
+    both = jnp.where(to_core == 0, jnp.broadcast_to(tokens, shape), jnp.broadcast_to(out_grad, shape))
     both = both.reshape((n_z * n_core,) + tokens.shape)
     mine = lax.all_to_all(both, ROW, 0, 0, tiled=True)
     mine = mine.reshape((1, -1) + tokens.shape[1:])

time: 172 us -> 172 us (level)
  no operation moved by 1% of the time
where the time goes in v11:
time: 172 us
  blocking collectives  129 us (75%)
  waiting for transfers between devices  26.2 us (15%)
  matrix products  6.02 us (4%)
  starting transfers between devices  5.2 us (3%)
  other arithmetic  3.43 us (2%)
    all_to_all x1, blocking collectives, gather_rows(): mine = lax.all_to_all(both, ROW, 0, 0, tiled=True)  47.3 us
    all_to_all x1, blocking collectives, body(): parts = lax.all_to_all(parts, 'col', 0, 0, tiled=True)  46.8 us
    all_to_all x1, waiting for transfers between devices, body(): input_grad = lax.all_to_all(total, 'z', 0, 0, tiled=True).sum(axis=0)  26.2 us
    all_to_all x1, blocking collectives, body(): spread = lax.all_to_all(spread, 'col', 0, 0, tiled=True)  25.2 us
    all_to_all x1, starting transfers between devices, body(): input_grad = lax.all_to_all(total, 'z', 0, 0, tiled=True).sum(axis=0)  5.2 us
    all_to_all x1, blocking collectives, gather_rows(): full = lax.all_to_all(mine, 'core', 0, 0, tiled=True)  4.71 us
    all_to_all x1, blocking collectives, body(): total = lax.all_to_all(total, 'core', 0, 0, tiled=True)  4.71 us
  transfers between devices with their start and end apart: 1, of which 1 were waited for; matrix products, arithmetic and copies ran while one was open for 2% of the time, Pallas kernels for 0%

profile of v11, /device:TPU:32, one launch (start us, length us, event | category | flops | bytes accessed | tf_op | source)
XLA Modules:
  0.0 171.9 jit_solution(6481545278351105904)
XLA Ops:
  0.6 0.0 copy-start
  0.7 0.1 iota.12
  0.8 0.9 broadcast_select_fusion
  1.6 47.3 %all_to_all.30 = bf16[32,16,512]{2,1,0:T(8,128)(2,1)S(1)} all-to-all(bf16[32,16,512]{2,1,0:T(8,128)(2,1)S(1)} %broadcast_select_fusion), channel_id=1, replica_groups=mesh['z'=16,'core'=2,'col'=16] {'z','core'}, dimensions={0} | all-to-all | bytes 1048576 | tf_op jit(solution)/shard_map/all_to_all | solution.py:24
  49.0 0.0 copy-start.1
  49.0 0.1 broadcast_in_dim.22
  49.1 4.7 %all_to_all.31 = bf16[2,512,512]{2,1,0:T(8,128)(2,1)S(1)} all-to-all(bf16[2,512,512]{2,1,0:T(8,128)(2,1)S(1)} %broadcast_in_dim.22), channel_id=1, replica_groups=mesh['z'=16,'core'=2,'col'=16] {'core'}, dimensions={0} | all-to-all | bytes 2097152 | tf_op jit(solution)/shard_map/all_to_all | solution.py:27
  53.8 0.0 copy-start.4
  53.8 0.1 fusion.12
  53.8 0.0 copy-done.1
  53.9 0.4 convolution_bitcast_fusion.1
  54.3 0.0 copy-done
  54.3 0.4 convolution_bitcast_fusion.2
  54.7 0.1 copy-done.4
  54.8 0.5 convolution_bitcast_fusion
  55.3 0.5 pad_maximum_fusion
  55.8 46.8 %all_to_all.32 = f32[16,3,32,512]{3,2,1,0:T(8,128)S(1)} all-to-all(f32[16,3,32,512]{3,2,1,0:T(8,128)S(1)} %pad_maximum_fusion), channel_id=1, replica_groups=mesh['z'=16,'core'=2,'col'=16] {'col'}, dimensions={0} | all-to-all | bytes 6291456 | tf_op jit(solution)/shard_map/all_to_all | solution.py:48
  102.6 0.4 bitcast_reduce_fusion
  103.0 0.1 reduce_sum.28
  103.1 0.2 broadcast_in_dim.23
  103.3 25.2 %all_to_all.33 = bf16[16,3,32,512]{3,2,1,0:T(8,128)(2,1)S(1)} all-to-all(bf16[16,3,32,512]{3,2,1,0:T(8,128)(2,1)S(1)} %broadcast_in_dim.23), channel_id=1, replica_groups=mesh['z'=16,'core'=2,'col'=16] {'col'}, dimensions={0} | all-to-all | bytes 3145728 | tf_op jit(solution)/shard_map/all_to_all | solution.py:53
  128.5 0.9 fusion.11
  129.4 0.0 copy-start.2
  129.4 0.5 fusion.13
  129.9 0.5 convolution_add_fusion
  130.4 0.1 copy.11
  130.5 0.0 copy-done.2
  130.5 0.0 copy-start.3
  130.5 4.7 %all_to_all.34 = f32[2,16,16,512]{3,2,1,0:T(8,128)S(1)} all-to-all(f32[2,16,16,512]{3,2,1,0:T(8,128)S(1)} %bitcast.52), channel_id=1, replica_groups=mesh['z'=16,'core'=2,'col'=16] {'core'}, dimensions={0} | all-to-all | bytes 2097152 | tf_op jit(solution)/shard_map/all_to_all | solution.py:70
  135.2 0.9 fusion
  136.1 5.2 %all-to-all-start.5 = ((f32[16,16,512]{2,1,0:T(8,128)}), f32[16,16,512]{2,1,0:T(8,128)S(1)}, u32[]{:S(2)}, u32[]{:S(2)}) async-start(f32[16,16,512]{2,1,0:T(8,128)} %fusion), calls=%async_computation.5 | async-start | bytes 1048576 | tf_op jit(solution)/shard_map/all_to_all | solution.py:72
  141.3 0.0 copy-done.3
  141.3 0.0 copy-start.5
  141.3 1.3 convolution_convert_fusion.1
  142.5 1.3 convolution_convert_fusion.2
  143.8 0.0 copy-done.5
  143.8 1.3 convolution_convert_fusion
  145.0 26.2 %all-to-all-done.5 = f32[16,16,512]{2,1,0:T(8,128)S(1)} async-done(((f32[16,16,512]{2,1,0:T(8,128)}), f32[16,16,512]{2,1,0:T(8,128)S(1)}, u32[]{:S(2)}, u32[]{:S(2)}) %all-to-all-start.5) | async-done | bytes 524320 | tf_op jit(solution)/shard_map/all_to_all | solution.py:72
  171.3 0.6 reduce_sum.29
  (4 shorter events, 0.1 us)
Async XLA Ops:
  0.6 53.7 %copy-start = (bf16[512,512]{1,0:T(8,128)(2,1)S(1)}, bf16[512,512]{1,0:T(8,128)(2,1)}, u32[]{:S(2)}) copy-start(bf16[512,512]{1,0:T(8,128)(2,1)} %param.7) | copy-start | bytes 1572868
  49.0 4.9 %copy-start.1 = (bf16[512,512]{1,0:T(8,128)(2,1)S(1)}, bf16[512,512]{1,0:T(8,128)(2,1)}, u32[]{:S(2)}) copy-start(bf16[512,512]{1,0:T(8,128)(2,1)} %param.8) | copy-start | bytes 1572868
  53.8 1.0 copy-start.4
  129.4 1.1 copy-start.2
  130.5 10.8 %copy-start.3 = (bf16[1,16,32,512]{3,2,0,1:T(8,128)(2,1)S(1)}, bf16[1,16,32,512]{3,2,0,1:T(8,128)(2,1)}, u32[]{:S(2)}) copy-start(bf16[1,16,32,512]{3,2,0,1:T(8,128)(2,1)} %copy-done.2) | copy-start | bytes 1572868
  136.1 35.2 %all-to-all-start.5 = ((f32[16,16,512]{2,1,0:T(8,128)}), f32[16,16,512]{2,1,0:T(8,128)S(1)}, u32[]{:S(2)}, u32[]{:S(2)}) async-start(f32[16,16,512]{2,1,0:T(8,128)} %fusion), calls=%async_computation.5 | async-start | bytes 1048576 | tf_op jit(solution)/shard_map/all_to_all | solution.py:72
  141.3 2.5 %copy-start.5 = (bf16[1,16,32,512]{3,2,0,1:T(8,128)(2,1)S(1)}, bf16[1,16,32,512]{3,2,0,1:T(8,128)(2,1)}, u32[]{:S(2)}) copy-start(bf16[1,16,32,512]{3,2,0,1:T(8,128)(2,1)} %get-tuple-element.4) | copy-start | bytes 1572868
